TPU v7x, 32 devices: a whole 2x2x4 slice. The times are simulated.
32 devices in a mesh: groups: 2 (over y), cam: 4 (over z), tm: 2 (over x), chan: 2 (over core).
Axes of the slice: x: 2, y: 2, z: 4, core: 2. Of those that a mesh axis runs over, the one named last changes fastest.
Arguments:
- video: bfloat16 [16, 8, 16, 8, 256], P(('groups', 'cam'), 'tm', None, None, 'chan'), parts along dimension 0, may hold values from -6 to 6
- conv_weight: bfloat16 [27, 256, 256], P(None, None, 'chan'), may hold values from -0.078125 to 0.078125
- proj_weight: bfloat16 [256, 16], P('chan'), may hold values from -0.375 to 0.375
- rig_sizes: int32 [8], P('groups'), parts along dimension 0, may hold values from 1 to 3, as said below
- camera_order: int32 [16], P('groups'), parts along dimension 0, may hold values from 0 to 7, as said below
- owner_slot: int32 [8], P('groups'), parts along dimension 0, may hold values from 0 to 3, as said below
- cotangent: bfloat16 [8, 8, 16, 128], P(('groups', 'cam'), 'tm'), parts along dimension 0, may hold values from -6 to 6
Outputs:
- robot_latent: float32 [8, 8, 16, 128], P(('groups', 'cam'), 'tm'), parts along dimension 0
- grad_conv: bfloat16 [54, 256, 256], P('groups', None, 'chan'), parts along dimension 0
- grad_proj: float32 [512, 16], P(('groups', 'chan')), parts along dimension 0
- grad_video: bfloat16 [16, 8, 16, 8, 256], P(('groups', 'cam'), 'tm', None, None, 'chan'), parts along dimension 0
There are 2 independent parts, one for each index of `groups`. A program takes and returns all parts, laid end to end along the dimension named above; an argument that names none is the same for every part. Nothing has to cross between parts.
Inputs may be any that keep to these rules, and one draw needn't show every extreme that they name: `rig_sizes`: the sizes sum to 8; the largest is exactly 3. `camera_order`: A permutation; the cameras whose places fall from rig_sizes[0] + ... + rig_sizes[r-1] to below rig_sizes[0] + ... + rig_sizes[r] belong to robot r. `owner_slot`: A permutation of the output rows.
All inputs are finite; a program needn't handle non-finite values.
Results may differ from a plain program's by a relative error of at most 0.0059.
Values may be sent and summed in bfloat16 or wider, within the bound.
No kernel may reach another device: no remote copies, remote signals or barrier semaphores. Data moves between devices by JAX's collectives and lax.ppermute only.
A program may use at most 128 MiB of HBM per device.

v0:
```python
import jax
import jax.numpy as jnp
from jax import lax
from jax.sharding import PartitionSpec as P

KT = 3
KS = 3


def shifted(shard, axis, by):
    size = lax.axis_size(axis)
    pairs = [(i, i + by) for i in range(size) if 0 <= i + by < size]
    return lax.ppermute(shard, axis, pairs)


def gathered(block, axis):
    size = lax.axis_size(axis)
    if size & (size - 1):
        return lax.all_gather(block, axis, axis=0, tiled=True)
    index = lax.axis_index(axis)
    blocks = block
    step = 1
    while step < size:
        pairs = [(i, i ^ step) for i in range(size)]
        other = lax.ppermute(blocks, axis, pairs)
        upper = (index & step) != 0
        blocks = jnp.where(
            upper,
            jnp.concatenate([other, blocks], axis=0),
            jnp.concatenate([blocks, other], axis=0),
        )
        step *= 2
    return blocks


def conv3d(lhs, rhs, padding, specs):
    return lax.conv_general_dilated(
        lhs,
        rhs,
        window_strides=(1, 1, 1),
        padding=padding,
        dimension_numbers=specs,
        preferred_element_type=jnp.float32,
    )


def weight_grad_sliced(whole_now, dpre5, space_pad):
    axes = ("cam", "tm")
    cams = lax.axis_size("cam")
    times = lax.axis_size("tm")
    count = cams * times
    cam_dev, frames, height, width, chans = whole_now.shape
    piece = chans // count
    chunks = whole_now.reshape(cam_dev, frames, height, width, count, piece)
    chunks = jnp.moveaxis(chunks, 4, 0)
    mine = lax.all_to_all(chunks, axes, 0, 0, tiled=True)
    mine = mine.reshape(cams, times, cam_dev, frames, height, width, piece)
    tail = mine[:, : times - 1, :, frames - (KT - 1) :]
    head = jnp.zeros((cams, 1) + tail.shape[2:], mine.dtype)
    before = jnp.concatenate([head, tail], axis=1)
    timed_all = jnp.concatenate([before, mine], axis=3)
    timed_all = timed_all.reshape(count * cam_dev, frames + KT - 1, height, width, piece)
    dpre_all = lax.all_gather(dpre5, axes, axis=0, tiled=True)
    part = conv3d(timed_all, dpre_all, space_pad, ("CDHWN", "IDHWO", "DHWNC"))
    part = part.astype(jnp.bfloat16)
    return lax.all_gather(part, axes, axis=3, tiled=True)


def joining_matrix(rig_sizes, camera_order, owner_slot):
    robots = rig_sizes.shape[0]
    ends = jnp.cumsum(rig_sizes)
    robot_of = jnp.sum((ends[None, :] <= camera_order[:, None]).astype(jnp.int32), axis=1)
    member = robot_of[:, None] == jnp.arange(robots, dtype=jnp.int32)[None, :]
    slot_of = jnp.sum(jnp.where(member, owner_slot[None, :], 0), axis=1)
    count_of = jnp.sum(jnp.where(member, rig_sizes[None, :], 0), axis=1)
    share = 1.0 / count_of.astype(jnp.float32)
    placed = slot_of[None, :] == jnp.arange(robots, dtype=jnp.int32)[:, None]
    return jnp.where(placed, share[None, :], jnp.zeros_like(share)[None, :])


def body(video, conv_weight, proj_weight, rig_sizes, camera_order, owner_slot, cotangent):
    cam_dev, frames, height, width, half_chan = video.shape
    pad_half = KS // 2
    lat_width = proj_weight.shape[1]
    out_half = conv_weight.shape[2]
    whole_now = lax.all_gather(video, "chan", axis=4, tiled=True)
    whole_cache = shifted(whole_now[:, frames - (KT - 1) :], "tm", 1)
    timed = jnp.concatenate([whole_cache, whole_now], axis=1)
    kernel = conv_weight.reshape(KT, KS, KS, conv_weight.shape[1], out_half)
    space_pad = [(0, 0), (pad_half, pad_half), (pad_half, pad_half)]
    pre5 = conv3d(timed, kernel, space_pad, ("NDHWC", "DHWIO", "NDHWC"))
    pre = pre5.reshape(-1, out_half)
    sigma = jax.nn.sigmoid(pre)
    act = (pre * sigma).astype(jnp.bfloat16)
    latent_part = jnp.dot(act, proj_weight, preferred_element_type=jnp.float32)
    latent = lax.psum(latent_part, "chan").astype(jnp.bfloat16)
    mixing = joining_matrix(rig_sizes, camera_order, owner_slot)
    cam_index = lax.axis_index("cam")
    my_row = lax.dynamic_slice_in_dim(mixing, cam_index, 1, 0)
    latent_maps = latent.reshape(cam_dev, frames, height, width * lat_width)
    block_in = gathered(latent_maps, "cam")
    flat_in = block_in.reshape(block_in.shape[0], -1).astype(jnp.float32)
    added = jnp.dot(
        my_row, flat_in, precision=lax.Precision.HIGHEST, preferred_element_type=jnp.float32
    )
    robot_latent = added.reshape(1, frames, height, width * lat_width)
    my_cols = lax.dynamic_slice_in_dim(mixing, cam_index * cam_dev, cam_dev, 1)
    block_in = gathered(cotangent, "cam")
    flat_in = block_in.reshape(block_in.shape[0], -1).astype(jnp.float32)
    spread = lax.dot_general(
        my_cols,
        flat_in,
        (((0,), (0,)), ((), ())),
        precision=lax.Precision.HIGHEST,
        preferred_element_type=jnp.float32,
    )
    dlatent = spread.astype(jnp.bfloat16).reshape(-1, lat_width)
    grad_proj_local = lax.dot_general(
        act, dlatent, (((0,), (0,)), ((), ())), preferred_element_type=jnp.float32
    )
    dact = lax.dot_general(
        dlatent, proj_weight, (((1,), (1,)), ((), ())), preferred_element_type=jnp.float32
    )
    dpre = (dact * sigma * (1.0 + pre * (1.0 - sigma))).astype(jnp.bfloat16)
    dpre5 = dpre.reshape(cam_dev, frames, height, width, out_half)
    if lax.axis_size("cam") * lax.axis_size("tm") <= 8:
        grad_conv = weight_grad_sliced(whole_now, dpre5, space_pad).reshape(
            KT * KS * KS, -1, out_half
        )
    else:
        grad_conv_local = conv3d(timed, dpre5, space_pad, ("CDHWN", "IDHWO", "DHWNC"))
        grad_conv_local = grad_conv_local.reshape(KT * KS * KS, -1, out_half)
        grad_conv_part = lax.psum_scatter(
            grad_conv_local, ("cam", "tm"), scatter_dimension=1, tiled=True
        )
        grad_conv = lax.all_gather(
            grad_conv_part.astype(jnp.bfloat16), ("cam", "tm"), axis=1, tiled=True
        )
    grad_proj = jnp.sum(gathered(gathered(grad_proj_local[None], "tm"), "cam"), axis=0)
    flipped = kernel[::-1, ::-1, ::-1]
    back_pad = [(KT - 1, KT - 1), (pad_half, pad_half), (pad_half, pad_half)]
    full_back = conv3d(dpre5, flipped, back_pad, ("NDHWC", "DHWOI", "NDHWC"))
    incoming = shifted(full_back[:, : KT - 1], "tm", -1)
    own_part = full_back[:, KT - 1 :]
    own_part = own_part.at[:, frames - (KT - 1) :].add(incoming)
    rounded = own_part.astype(jnp.bfloat16)
    chan_count = lax.axis_size("chan")
    chan_index = lax.axis_index("chan")
    width_out = rounded.shape[4] // chan_count
    summed = lax.dynamic_slice_in_dim(rounded, chan_index * width_out, width_out, 4).astype(
        jnp.float32
    )
    for step in range(1, chan_count):
        target = (chan_index + step) % chan_count
        sent = lax.dynamic_slice_in_dim(rounded, target * width_out, width_out, 4)
        pairs = [(i, (i + step) % chan_count) for i in range(chan_count)]
        summed = summed + lax.ppermute(sent, "chan", pairs).astype(jnp.float32)
    grad_video = summed.astype(jnp.bfloat16)
    return (robot_latent, grad_conv, grad_proj, grad_video)


def solution(mesh):
    return jax.shard_map(
        body,
        mesh=mesh,
        in_specs=(
            P(("groups", "cam"), "tm", None, None, "chan"),
            P(None, None, "chan"),
            P("chan", None),
            P("groups"),
            P("groups"),
            P("groups"),
            P(("groups", "cam"), "tm", None, None),
        ),
        out_specs=(
            P(("groups", "cam"), "tm", None, None),
            P("groups", None, "chan"),
            P(("groups", "chan"), None),
            P(("groups", "cam"), "tm", None, None, "chan"),
        ),
        check_vma=False,
    )
```

profile of v0, /device:TPU:0, one launch (start us, length us, event | category | flops | bytes accessed | tf_op | source)
XLA Modules:
  0.0 165.5 jit_solution(4598057590557564718)
XLA Ops:
  7.2 1.3 copy.49
  8.6 2.3 %all_gather.9 = bf16[2,4,16,8,256]{4,0,3,2,1:T(2,128)(2,1)S(1)} all-gather(bf16[2,4,16,8,128]{4,0,3,2,1:T(2,128)(2,1)S(1)} %copy.49), channel_id=1, replica_groups=mesh['groups'=2,'cam'=4,'tm'=2,'chan'=2] {'chan'}, dimensions={4}, use_global_device_ids=true | all-gather | bytes 786432 | tf_op jit(solution)/shard_map/all_gather | solution.py:86
  10.9 0.2 slice.52
  11.1 4.7 %collective-permute-start = (bf16[2,2,16,8,256]{4,0,3,2,1:T(2,128)(2,1)S(1)}, bf16[2,2,16,8,256]{4,0,3,2,1:T(2,128)(2,1)S(1)}, u32[]{:S(2)}, u32[]{:S(2)}) collective-permute-start(bf16[2,2,16,8,256]{4,0,3,2,1:T(2,128)(2,1)S(1)} %slice.52), channel_id=1, source_target_pairs={{0,2},{1,3},{4,6},{5,7},{8,10},{9,11},{12,14},{13,15},{16,18},{17,... | collective-permute-start | bytes 786440 | tf_op jit(solution)/shard_map/ppermute | solution.py:13
  15.8 1.6 collective-permute-start.3
  17.4 0.8 reduce-window.8
  18.3 0.7 convert_reduce_fusion
  19.0 0.8 select_reduce_fusion.1
  19.8 0.7 copy.86
  20.6 0.8 maximum_select_fusion.6
  21.4 2.6 %collective-permute-start.4 = (bf16[2,4,16,128]{3,2,1,0:T(8,128)(2,1)S(1)}, bf16[2,4,16,128]{3,2,1,0:T(8,128)(2,1)S(1)}, u32[]{:S(2)}, u32[]{:S(2)}) collective-permute-start(bf16[2,4,16,128]{3,2,1,0:T(8,128)(2,1)S(1)} %maximum_select_fusion.6), channel_id=1, source_target_pairs={{0,8},{4,12},{8,0},{12,4},{1,9},{5,13},{9,1},{13,5},{2,10},{6,14},... | collective-permute-start | bytes 98312 | tf_op jit(solution)/shard_map/ppermute | solution.py:25
  24.0 0.2 broadcast_select_fusion
  24.1 2.1 %collective-permute-done.4 = bf16[2,4,16,128]{3,2,1,0:T(8,128)(2,1)S(1)} collective-permute-done((bf16[2,4,16,128]{3,2,1,0:T(8,128)(2,1)S(1)}, bf16[2,4,16,128]{3,2,1,0:T(8,128)(2,1)S(1)}, u32[]{:S(2)}, u32[]{:S(2)}) %collective-permute-start.4) | collective-permute-done | bytes 32800 | tf_op jit(solution)/shard_map/ppermute | solution.py:25
  26.3 0.4 convolution_convert_fusion
  26.7 0.2 reshape.152
  26.9 6.6 %fusion.12 = f32[2,4,16,8,128]{4,0,3,2,1:T(2,128)S(1)} fusion(bf16[3,3,3,256,128]{4,3,2,1,0:T(8,128)(2,1)S(1)} %bitcast.87, bf16[2,4,16,8,256]{4,0,3,2,1:T(2,128)(2,1)S(1)} %all_gather.9, bf16[2,2,16,8,256]{4,0,3,2,1:T(2,128)(2,1)S(1)} %collective-permute-done), kind=kOutput, calls=%fused_computation.13 | convolution fusion | flops 1593311232 | bytes 3080192 | tf_op jit(solution)/shard_map/conv_general_dilated | solution.py:37
  33.5 0.2 multiply_convert_fusion
  33.7 0.2 fusion.16
  33.9 0.3 copy-done.2
  34.2 0.9 fusion.6
  35.1 2.2 %reshape.150 = bf16[2,4,16,8,8,32]{5,4,0,3,2,1:T(8,128)(2,1)} reshape(bf16[2,4,16,8,256]{4,0,3,2,1:T(2,128)(2,1)S(1)} %all_gather.9) | data formatting | bytes 1048576 | tf_op jit(solution)/shard_map/reshape | solution.py:54
  37.4 5.1 %copy.90 = bf16[2,4,16,8,8,32]{5,0,3,2,1,4:T(2,128)(2,1)} copy(bf16[2,4,16,8,8,32]{5,4,0,3,2,1:T(8,128)(2,1)} %reshape.150) | data formatting | bytes 1048576 | tf_op jit(solution)/shard_map/reshape | solution.py:54
  42.5 6.0 %reshape.157 = bf16[8,2,16384]{2,1,0:T(2,128)(2,1)} reshape(bf16[8,4,16,8,2,32]{5,4,3,2,1,0:T(2,128)(2,1)} %bitcast.91) | data formatting | bytes 1048576
  48.4 4.1 %all-to-all-start = ((bf16[8,2,16384]{2,1,0:T(2,128)(2,1)}), bf16[8,2,16384]{2,1,0:T(2,128)(2,1)S(1)}, u32[]{:S(2)}, u32[]{:S(2)}) async-start(bf16[8,2,16384]{2,1,0:T(2,128)(2,1)} %reshape.157), calls=%async_computation | async-start | bytes 1048576 | tf_op jit(solution)/shard_map/all_to_all | solution.py:56
  52.7 0.2 convolution_bitcast_fusion
  52.9 2.0 %collective-permute-start.5 = (f32[1,128,16]{1,2,0:T(8,128)S(1)}, f32[1,128,16]{1,2,0:T(8,128)S(1)}, u32[]{:S(2)}, u32[]{:S(2)}) collective-permute-start(f32[1,128,16]{1,2,0:T(8,128)S(1)} %convolution_bitcast_fusion), channel_id=1, source_target_pairs={{0,2},{2,0},{1,3},{3,1},{4,6},{6,4},{5,7},{7,5},{8,10},{10,8},{9,1... | collective-permute-start | bytes 24584 | tf_op jit(solution)/shard_map/ppermute | solution.py:25
  54.9 8.1 %fusion.19 = f32[2,6,16,8,256]{4,0,3,2,1:T(2,128)} fusion(bf16[3,3,3,256,128]{4,3,2,1,0:T(8,128)(2,1)S(1)} %bitcast.88, bf16[2,4,16,8,128]{4,3,2,1,0:T(8,128)(2,1)S(1)} %bitcast.97), kind=kOutput, calls=%fused_computation.26 | convolution fusion | flops 1591738368 | bytes 3604480 | tf_op jit(solution)/shard_map/conv_general_dilated | solution.py:37
  63.0 4.7 %all-to-all-done = bf16[8,2,16384]{2,1,0:T(2,128)(2,1)S(1)} async-done(((bf16[8,2,16384]{2,1,0:T(2,128)(2,1)}), bf16[8,2,16384]{2,1,0:T(2,128)(2,1)S(1)}, u32[]{:S(2)}, u32[]{:S(2)}) %all-to-all-start) | async-done | bytes 524320 | tf_op jit(solution)/shard_map/all_to_all | solution.py:56
  67.7 2.0 %reshape.158 = bf16[8,4,16,8,2,32]{5,4,3,2,1,0:T(2,128)(2,1)} reshape(bf16[8,2,16384]{2,1,0:T(2,128)(2,1)S(1)} %all-to-all-done) | data formatting | bytes 1048576
  69.7 5.2 %copy.55 = bf16[8,2,4,16,8,32]{5,1,0,4,3,2:T(2,128)(2,1)} copy(bf16[8,2,4,16,8,32]{5,1,4,3,2,0:T(2,128)(2,1)} %bitcast.89) | data formatting | bytes 1048576 | tf_op jit(solution)/shard_map/all_to_all | solution.py:56
  74.9 1.4 slice.53
  76.3 0.5 copy.63
  76.9 2.3 %concatenate.96 = bf16[4,2,2,2,16,8,32]{6,2,1,0,5,4,3:T(2,128)(2,1)} pad(bf16[4,1,2,2,16,8,32]{6,2,1,0,5,4,3:T(2,128)(2,1)S(1)} %copy.63, bf16[]{:T(256)} %constant.67.clone.1), padding=0_0x1_0x0_0x0_0x0_0x0_0x0_0 | pad | bytes 393218 | tf_op jit(solution)/shard_map/concatenate | solution.py:60
  79.1 9.4 %all-gather.3.cloned.1.call-done = bf16[16,4,16,8,128]{4,3,2,1,0:T(8,128)(2,1)} async-done(((bf16[2,4,16,8,128]{4,3,2,1,0:T(8,128)(2,1)}), bf16[16,4,16,8,128]{4,3,2,1,0:T(8,128)(2,1)}) %all-gather.3.cloned.1.call-update) | async-done | bytes 2097168 | tf_op jit(solution)/shard_map/all_gather | solution.py:63
  88.6 16.9 %fusion.7 = bf16[3,3,3,32,128]{4,3,2,1,0:T(8,128)(2,1)} fusion(bf16[16,4,16,8,128]{4,3,2,1,0:T(8,128)(2,1)} %all-gather.3.cloned.1.call-done, bf16[16,4,16,8,32]{4,0,3,2,1:T(8,128)(2,1)} %bitcast.92, bf16[16,2,16,8,32]{4,0,3,2,1:T(8,128)(2,1)} %bitcast.95), kind=kOutput, calls=%fused_computation.10 | convolution fusion | flops 1593421824 | bytes 3104768 | tf_op jit(solution)/shard_map/conv_general_dilated | solution.py:37
  105.5 0.2 fusion.38
  105.7 1.6 collective-permute-start.6
  107.2 3.6 %psum.7 = bf16[1024,16]{0,1:T(8,128)(2,1)S(1)} all-reduce(f32[1024,16]{0,1:T(8,128)S(1)} %fusion.38), channel_id=1, replica_groups=mesh['groups'=2,'cam'=4,'tm'=2,'chan'=2] {'chan'}, use_global_device_ids=true, to_apply=%region_4.5 | all-reduce | flops 16384 | bytes 98304 | tf_op jit(solution)/shard_map/psum | solution.py:96
  110.8 0.2 copy.51
  111.0 0.3 concatenate.91
  111.3 0.2 reshape.148
  111.5 1.6 slice.54
  113.1 1.2 slice.56
  114.4 0.6 collective-permute-start.1
  115.0 1.3 collective-permute-start.8
  116.3 1.9 %collective-permute-start.7 = (f32[4,128,16]{1,2,0:T(8,128)S(1)}, f32[4,128,16]{1,2,0:T(8,128)S(1)}, u32[]{:S(2)}, u32[]{:S(2)}) collective-permute-start(f32[4,128,16]{1,2,0:T(8,128)S(1)} %maximum_select_fusion.7), channel_id=1, source_target_pairs={{0,8},{4,12},{8,0},{12,4},{1,9},{5,13},{9,1},{13,5},{2,10},{6,14},... | collective-permute-start | bytes 98312 | tf_op jit(solution)/shard_map/ppermute | solution.py:25
  118.2 0.3 collective-permute-done.1
  118.5 1.5 collective-permute-start.2
  119.9 0.1 maximum_select_fusion.2
  120.1 4.3 %collective-permute-done.7 = f32[4,128,16]{1,2,0:T(8,128)S(1)} collective-permute-done((f32[4,128,16]{1,2,0:T(8,128)S(1)}, f32[4,128,16]{1,2,0:T(8,128)S(1)}, u32[]{:S(2)}, u32[]{:S(2)}) %collective-permute-start.7) | collective-permute-done | bytes 32800 | tf_op jit(solution)/shard_map/ppermute | solution.py:25
  124.4 0.6 fusion.26
  125.0 3.6 %collective-permute-done.2 = bf16[4,4,16,128]{3,2,1,0:T(8,128)(2,1)S(1)} collective-permute-done((bf16[4,4,16,128]{3,2,1,0:T(8,128)(2,1)S(1)}, bf16[4,4,16,128]{3,2,1,0:T(8,128)(2,1)S(1)}, u32[]{:S(2)}, u32[]{:S(2)}) %collective-permute-start.2) | collective-permute-done | bytes 65568 | tf_op jit(solution)/shard_map/ppermute | solution.py:25
  128.6 0.1 copy.85
  128.7 2.1 %collective-permute-done.8 = f32[2,2,16,8,256]{4,0,3,2,1:T(2,128)S(1)} collective-permute-done((f32[2,2,16,8,256]{4,0,3,2,1:T(2,128)S(1)}, f32[2,2,16,8,256]{4,0,3,2,1:T(2,128)S(1)}, u32[]{:S(2)}, u32[]{:S(2)}) %collective-permute-start.8) | collective-permute-done | bytes 524320 | tf_op jit(solution)/shard_map/ppermute | solution.py:13
  130.8 1.4 fusion.13
  132.1 0.2 constant_dynamic-slice_fusion
  132.3 0.1 collective-permute-start.9
  132.4 0.1 maximum_select_fusion
  132.6 0.9 fusion.32
  133.4 0.5 collective-permute-done.9
  133.9 0.3 add_convert_fusion
  134.2 0.7 copy.60
  135.0 20.8 %all-gather.5.cloned.1.call-done = bf16[3,3,3,256,128]{4,3,2,1,0:T(8,128)(2,1)} async-done(((bf16[3,3,3,32,128]{4,3,2,1,0:T(8,128)(2,1)}), bf16[3,3,3,256,128]{4,3,2,1,0:T(8,128)(2,1)}) %all-gather.5.cloned.1.call-update) | async-done | bytes 1769488 | tf_op jit(solution)/shard_map/all_gather | solution.py:66
  155.8 2.9 %copy.93 = bf16[27,256,128]{2,1,0:T(8,128)(2,1)} copy(bf16[27,256,128]{2,1,0:T(8,128)(2,1)} %bitcast.93) | data formatting | bytes 3538944
  (21 shorter events, 0.3 us)
Async XLA Ops:
  7.2 19.8 %copy-start = (bf16[27,256,128]{2,1,0:T(8,128)(2,1)S(1)}, bf16[27,256,128]{2,1,0:T(8,128)(2,1)}, u32[]{:S(2)}) copy-start(bf16[27,256,128]{2,1,0:T(8,128)(2,1)} %param.10) | copy-start | bytes 5308420
  7.2 81.4 %all-gather.3.cloned.1.call-start = ((), (), s32[]{:S(2)}) async-start(), calls=%async_computation.1 | async-start | bytes 2359296 | tf_op jit(solution)/shard_map/all_gather | solution.py:63
  11.1 15.8 %collective-permute-start = (bf16[2,2,16,8,256]{4,0,3,2,1:T(2,128)(2,1)S(1)}, bf16[2,2,16,8,256]{4,0,3,2,1:T(2,128)(2,1)S(1)}, u32[]{:S(2)}, u32[]{:S(2)}) collective-permute-start(bf16[2,2,16,8,256]{4,0,3,2,1:T(2,128)(2,1)S(1)} %slice.52), channel_id=1, source_target_pairs={{0,2},{1,3},{4,6},{5,7},{8,10},{9,11},{12,14},{13,15},{16,18},{17,... | collective-permute-start | bytes 786440 | tf_op jit(solution)/shard_map/ppermute | solution.py:13
  15.8 4.7 %collective-permute-start.3 = (bf16[1,4,16,128]{3,2,1,0:T(8,128)(2,1)}, bf16[1,4,16,128]{3,2,1,0:T(8,128)(2,1)S(1)}, u32[]{:S(2)}, u32[]{:S(2)}) collective-permute-start(bf16[1,4,16,128]{3,2,1,0:T(8,128)(2,1)} %param.15), channel_id=1, source_target_pairs={{0,4},{4,0},{8,12},{12,8},{1,5},{5,1},{9,13},{13,9},{2,6},{6,2},{1... | collective-permute-start | bytes 49160 | tf_op jit(solution)/shard_map/ppermute | solution.py:25
  21.4 4.8 %collective-permute-start.4 = (bf16[2,4,16,128]{3,2,1,0:T(8,128)(2,1)S(1)}, bf16[2,4,16,128]{3,2,1,0:T(8,128)(2,1)S(1)}, u32[]{:S(2)}, u32[]{:S(2)}) collective-permute-start(bf16[2,4,16,128]{3,2,1,0:T(8,128)(2,1)S(1)} %maximum_select_fusion.6), channel_id=1, source_target_pairs={{0,8},{4,12},{8,0},{12,4},{1,9},{5,13},{9,1},{13,5},{2,10},{6,14},... | collective-permute-start | bytes 98312 | tf_op jit(solution)/shard_map/ppermute | solution.py:25
  33.5 0.7 copy-start.2
  42.5 12.4 %copy-start.1 = (bf16[1024,128]{1,0:T(8,128)(2,1)S(1)}, bf16[1024,128]{1,0:T(8,128)(2,1)}, u32[]{:S(2)}) copy-start(bf16[1024,128]{1,0:T(8,128)(2,1)} %fusion.6) | copy-start | bytes 786436
  48.4 19.2 %all-to-all-start = ((bf16[8,2,16384]{2,1,0:T(2,128)(2,1)}), bf16[8,2,16384]{2,1,0:T(2,128)(2,1)S(1)}, u32[]{:S(2)}, u32[]{:S(2)}) async-start(bf16[8,2,16384]{2,1,0:T(2,128)(2,1)} %reshape.157), calls=%async_computation | async-start | bytes 1048576 | tf_op jit(solution)/shard_map/all_to_all | solution.py:56
  52.6 103.2 %all-gather.5.cloned.1.call-start = ((), (), s32[]{:S(2)}) async-start(), calls=%async_computation.2 | async-start | bytes 1990656 | tf_op jit(solution)/shard_map/all_gather | solution.py:66
  52.9 52.8 %collective-permute-start.5 = (f32[1,128,16]{1,2,0:T(8,128)S(1)}, f32[1,128,16]{1,2,0:T(8,128)S(1)}, u32[]{:S(2)}, u32[]{:S(2)}) collective-permute-start(f32[1,128,16]{1,2,0:T(8,128)S(1)} %convolution_bitcast_fusion), channel_id=1, source_target_pairs={{0,2},{2,0},{1,3},{3,1},{4,6},{6,4},{5,7},{7,5},{8,10},{10,8},{9,1... | collective-permute-start | bytes 24584 | tf_op jit(solution)/shard_map/ppermute | solution.py:25
  105.7 10.6 %collective-permute-start.6 = (f32[2,128,16]{1,2,0:T(8,128)S(1)}, f32[2,128,16]{1,2,0:T(8,128)S(1)}, u32[]{:S(2)}, u32[]{:S(2)}) collective-permute-start(f32[2,128,16]{1,2,0:T(8,128)S(1)} %maximum_select_fusion.8), channel_id=1, source_target_pairs={{0,4},{4,0},{8,12},{12,8},{1,5},{5,1},{9,13},{13,9},{2,6},{6,2},{1... | collective-permute-start | bytes 49160 | tf_op jit(solution)/shard_map/ppermute | solution.py:25
  114.4 4.0 %collective-permute-start.1 = (bf16[2,4,16,128]{3,2,1,0:T(8,128)(2,1)S(1)}, bf16[2,4,16,128]{3,2,1,0:T(8,128)(2,1)S(1)}, u32[]{:S(2)}, u32[]{:S(2)}) collective-permute-start(bf16[2,4,16,128]{3,2,1,0:T(8,128)(2,1)S(1)} %reshape.148), channel_id=1, source_target_pairs={{0,4},{4,0},{8,12},{12,8},{1,5},{5,1},{9,13},{13,9},{2,6},{6,2},{1... | collective-permute-start | bytes 98312 | tf_op jit(solution)/shard_map/ppermute | solution.py:25
  115.0 15.8 %collective-permute-start.8 = (f32[2,2,16,8,256]{4,0,3,2,1:T(2,128)S(1)}, f32[2,2,16,8,256]{4,0,3,2,1:T(2,128)S(1)}, u32[]{:S(2)}, u32[]{:S(2)}) collective-permute-start(f32[2,2,16,8,256]{4,0,3,2,1:T(2,128)S(1)} %slice.56), channel_id=1, source_target_pairs={{2,0},{3,1},{6,4},{7,5},{10,8},{11,9},{14,12},{15,13},{18,16},{19,... | collective-permute-start | bytes 1572872 | tf_op jit(solution)/shard_map/ppermute | solution.py:13
  116.3 8.1 %collective-permute-start.7 = (f32[4,128,16]{1,2,0:T(8,128)S(1)}, f32[4,128,16]{1,2,0:T(8,128)S(1)}, u32[]{:S(2)}, u32[]{:S(2)}) collective-permute-start(f32[4,128,16]{1,2,0:T(8,128)S(1)} %maximum_select_fusion.7), channel_id=1, source_target_pairs={{0,8},{4,12},{8,0},{12,4},{1,9},{5,13},{9,1},{13,5},{2,10},{6,14},... | collective-permute-start | bytes 98312 | tf_op jit(solution)/shard_map/ppermute | solution.py:25
  118.5 10.1 %collective-permute-start.2 = (bf16[4,4,16,128]{3,2,1,0:T(8,128)(2,1)S(1)}, bf16[4,4,16,128]{3,2,1,0:T(8,128)(2,1)S(1)}, u32[]{:S(2)}, u32[]{:S(2)}) collective-permute-start(bf16[4,4,16,128]{3,2,1,0:T(8,128)(2,1)S(1)} %maximum_select_fusion.1), channel_id=1, source_target_pairs={{0,8},{4,12},{8,0},{12,4},{1,9},{5,13},{9,1},{13,5},{2,10},{6,14},... | collective-permute-start | bytes 196616 | tf_op jit(solution)/shard_map/ppermute | solution.py:25
  132.3 1.6 collective-permute-start.9
Sparse Core Ops, SparseCore 0:
  35.3 53.2 all-gather.2
  105.6 50.1 all-gather.4
where the time goes:
time: 166 us
  waiting for transfers between devices  47.9 us (29%)
  local copies, waits for them, and re-layouts  35 us (21%)
  matrix products  34.1 us (21%)
  starting transfers between devices  22 us (13%)
  between operations  14.3 us (9%)
  other arithmetic  6.19 us (4%)
  blocking collectives  5.92 us (4%)
    conv_general_dilated x3, matrix products, conv3d(): lax.conv_general_dilated(lhs, rhs, window_strides=(1, 1, 1), padding=padd...  31.6 us
    all_gather x1, waiting for transfers between devices, weight_grad_sliced(): return lax.all_gather(part, axes, axis=3, tiled=True)  20.8 us
    unnamed x17, local copies, waits for them, and re-layouts  14.7 us
    ppermute x7, starting transfers between devices, gathered(): other = lax.ppermute(blocks, axis, pairs)  11.7 us
    ppermute x7, waiting for transfers between devices, gathered(): other = lax.ppermute(blocks, axis, pairs)  10.3 us
    all_gather x1, waiting for transfers between devices, weight_grad_sliced(): dpre_all = lax.all_gather(dpre5, axes, axis=0, tiled=True)  9.44 us
    reshape x2, local copies, waits for them, and re-layouts, weight_grad_sliced(): chunks = whole_now.reshape(cam_dev, frames, height, width, count, piece)  7.36 us
    ppermute x2, starting transfers between devices, shifted(): return lax.ppermute(shard, axis, pairs)  6.01 us
  transfers between devices with their start and end apart: 13, of which 9 were waited for; matrix products, arithmetic and copies ran while one was open for 38% of the time, Pallas kernels for 0%

commit v1 on v0

--- a/solution.py
+++ b/solution.py
@@ -66,6 +66,19 @@
     return lax.all_gather(part, axes, axis=3, tiled=True)
 
 
+def xor_gathered(block, axis):
+    size = lax.axis_size(axis)
+    if size & (size - 1):
+        return lax.all_gather(block, axis, axis=0, tiled=True), jnp.arange(size)
+    blocks = block
+    step = 1
+    while step < size:
+        pairs = [(i, i ^ step) for i in range(size)]
+        blocks = jnp.concatenate([blocks, lax.ppermute(blocks, axis, pairs)], axis=0)
+        step *= 2
+    return blocks, lax.axis_index(axis) ^ jnp.arange(size)
+
+
 def joining_matrix(rig_sizes, camera_order, owner_slot):
     robots = rig_sizes.shape[0]
     ends = jnp.cumsum(rig_sizes)
@@ -98,17 +111,23 @@
     cam_index = lax.axis_index("cam")
     my_row = lax.dynamic_slice_in_dim(mixing, cam_index, 1, 0)
     latent_maps = latent.reshape(cam_dev, frames, height, width * lat_width)
-    block_in = gathered(latent_maps, "cam")
+    block_in, source = xor_gathered(latent_maps, "cam")
     flat_in = block_in.reshape(block_in.shape[0], -1).astype(jnp.float32)
+    places = (source[:, None] * cam_dev + jnp.arange(cam_dev)[None, :]).reshape(-1)
     added = jnp.dot(
-        my_row, flat_in, precision=lax.Precision.HIGHEST, preferred_element_type=jnp.float32
+        my_row[:, places],
+        flat_in,
+        precision=lax.Precision.HIGHEST,
+        preferred_element_type=jnp.float32,
     )
     robot_latent = added.reshape(1, frames, height, width * lat_width)
     my_cols = lax.dynamic_slice_in_dim(mixing, cam_index * cam_dev, cam_dev, 1)
-    block_in = gathered(cotangent, "cam")
+    block_in, source = xor_gathered(cotangent, "cam")
     flat_in = block_in.reshape(block_in.shape[0], -1).astype(jnp.float32)
+    rows_per = cotangent.shape[0]
+    places = (source[:, None] * rows_per + jnp.arange(rows_per)[None, :]).reshape(-1)
     spread = lax.dot_general(
-        my_cols,
+        my_cols[places],
         flat_in,
         (((0,), (0,)), ((), ())),
         precision=lax.Precision.HIGHEST,

time: 166 us -> 163 us (0.982)
  waiting for transfers between devices: 47.9 us -> 45.1 us
    ppermute x7 -> x3, waiting for transfers between devices: 10.3 us -> 0.01 us  [gathered(): other = lax.ppermute(blocks, axis, pairs)]
    all_to_all x1, waiting for transfers between devices: 4.7 us -> 14.7 us  [weight_grad_sliced(): mine = lax.all_to_all(chunks, axes, 0, 0, tiled=True)]
    ppermute x7 -> x3, starting transfers between devices: 11.7 us -> 4.03 us  [gathered(): other = lax.ppermute(blocks, axis, pairs)]
    all_gather x1, waiting for transfers between devices: 20.8 us -> 13.8 us  [weight_grad_sliced(): return lax.all_gather(part, axes, axis=3, tiled=True)]
    ppermute x0 -> x4, waiting for transfers between devices: none -> 6.07 us  [xor_gathered(): lax.ppermute(blocks, axis, pairs)]
    ppermute x0 -> x4, starting transfers between devices: none -> 4.91 us  [xor_gathered(): lax.ppermute(blocks, axis, pairs)]
    ppermute x2, waiting for transfers between devices: 2.11 us -> 0.01 us  [shifted(): return lax.ppermute(shard, axis, pairs)]
    unnamed x17 -> x16, local copies, waits for them, and re-layouts: 14.7 us -> 15 us
  transfers between devices with their start and end apart: 13 -> 13, of which waited for: 9 -> 7; matrix products, arithmetic and copies ran while one was open for 38% -> 28% of each run, Pallas kernels for 0% -> 0%
where the time goes in v1:
time: 163 us; the launch traced here: 162 us
  waiting for transfers between devices  45.1 us (28%)
  local copies, waits for them, and re-layouts  36.3 us (22%)
  matrix products  33.5 us (21%)
  starting transfers between devices  20.4 us (13%)
  between operations  14.4 us (9%)
  other arithmetic  6.66 us (4%)
  blocking collectives  5.92 us (4%)
    conv_general_dilated x3, matrix products, conv3d(): lax.conv_general_dilated(lhs, rhs, window_strides=(1, 1, 1), padding=padd...  31 us
    unnamed x16, local copies, waits for them, and re-layouts  15 us
    all_to_all x1, waiting for transfers between devices, weight_grad_sliced(): mine = lax.all_to_all(chunks, axes, 0, 0, tiled=True)  14.7 us
    all_gather x1, waiting for transfers between devices, weight_grad_sliced(): return lax.all_gather(part, axes, axis=3, tiled=True)  13.8 us
    all_gather x1, waiting for transfers between devices, weight_grad_sliced(): dpre_all = lax.all_gather(dpre5, axes, axis=0, tiled=True)  9.97 us
    reshape x2, local copies, waits for them, and re-layouts, weight_grad_sliced(): chunks = whole_now.reshape(cam_dev, frames, height, width, count, piece)  7.18 us
    ppermute x4, waiting for transfers between devices, xor_gathered(): lax.ppermute(blocks, axis, pairs)  6.07 us
    ppermute x2, starting transfers between devices, shifted(): return lax.ppermute(shard, axis, pairs)  6.01 us
  transfers between devices with their start and end apart: 13, of which 7 were waited for; matrix products, arithmetic and copies ran while one was open for 28% of the time, Pallas kernels for 0%

profile of v1, /device:TPU:0, one launch (start us, length us, event | category | flops | bytes accessed | tf_op | source)
XLA Modules:
  0.0 162.2 jit_solution(16870228121008484841)
XLA Ops:
  7.2 1.3 copy.49
  8.6 2.3 %all_gather.9 = bf16[2,4,16,8,256]{4,0,3,2,1:T(2,128)(2,1)S(1)} all-gather(bf16[2,4,16,8,128]{4,0,3,2,1:T(2,128)(2,1)S(1)} %copy.49), channel_id=1, replica_groups=mesh['groups'=2,'cam'=4,'tm'=2,'chan'=2] {'chan'}, dimensions={4}, use_global_device_ids=true | all-gather | bytes 786432 | tf_op jit(solution)/shard_map/all_gather | solution.py:99
  10.9 0.2 slice.56
  11.1 4.7 %collective-permute-start = (bf16[2,2,16,8,256]{4,0,3,2,1:T(2,128)(2,1)S(1)}, bf16[2,2,16,8,256]{4,0,3,2,1:T(2,128)(2,1)S(1)}, u32[]{:S(2)}, u32[]{:S(2)}) collective-permute-start(bf16[2,2,16,8,256]{4,0,3,2,1:T(2,128)(2,1)S(1)} %slice.56), channel_id=1, source_target_pairs={{0,2},{1,3},{4,6},{5,7},{8,10},{9,11},{12,14},{13,15},{16,18},{17,... | collective-permute-start | bytes 786440 | tf_op jit(solution)/shard_map/ppermute | solution.py:13
  15.8 1.6 %collective-permute-start.3 = (bf16[1,4,16,128]{3,2,1,0:T(8,128)(2,1)}, bf16[1,4,16,128]{3,2,1,0:T(8,128)(2,1)S(1)}, u32[]{:S(2)}, u32[]{:S(2)}) collective-permute-start(bf16[1,4,16,128]{3,2,1,0:T(8,128)(2,1)} %param.15), channel_id=1, source_target_pairs={{0,4},{4,0},{8,12},{12,8},{1,5},{5,1},{9,13},{13,9},{2,6},{6,2},{1... | collective-permute-start | bytes 49160 | tf_op jit(solution)/shard_map/ppermute | solution.py:77
  17.4 0.8 reduce-window.8
  18.3 0.7 convert_reduce_fusion
  19.0 0.8 select_reduce_fusion.1
  19.8 0.7 pad_maximum_fusion.5
  20.6 2.6 %collective-permute-start.4 = (bf16[2,4,16,128]{3,2,1,0:T(8,128)(2,1)S(1)}, bf16[2,4,16,128]{3,2,1,0:T(8,128)(2,1)S(1)}, u32[]{:S(2)}, u32[]{:S(2)}) collective-permute-start(bf16[2,4,16,128]{3,2,1,0:T(8,128)(2,1)S(1)} %pad_maximum_fusion.5), channel_id=1, source_target_pairs={{0,8},{4,12},{8,0},{12,4},{1,9},{5,13},{9,1},{13,5},{2,10},{6,14},... | collective-permute-start | bytes 98312 | tf_op jit(solution)/shard_map/ppermute | solution.py:77
  23.1 0.1 constant_dynamic-slice_fusion.1
  23.2 0.6 gather_fusion.1
  23.8 1.6 collective-permute-done.4
  25.4 0.7 pad_maximum_fusion.4
  26.1 0.3 convolution_convert_fusion
  26.4 0.2 reshape.191
  26.7 6.6 %fusion.12 = f32[2,4,16,8,128]{4,0,3,2,1:T(2,128)S(1)} fusion(bf16[3,3,3,256,128]{4,3,2,1,0:T(8,128)(2,1)S(1)} %bitcast.82, bf16[2,4,16,8,256]{4,0,3,2,1:T(2,128)(2,1)S(1)} %all_gather.9, bf16[2,2,16,8,256]{4,0,3,2,1:T(2,128)(2,1)S(1)} %collective-permute-done), kind=kOutput, calls=%fused_computation.15 | convolution fusion | flops 1593311232 | bytes 3080192 | tf_op jit(solution)/shard_map/conv_general_dilated | solution.py:37
  33.2 0.2 multiply_convert_fusion
  33.4 0.2 fusion.16
  33.6 0.3 copy-done.3
  33.9 0.9 fusion.6
  34.9 2.0 %reshape.188 = bf16[2,4,16,8,8,32]{5,4,0,3,2,1:T(8,128)(2,1)} reshape(bf16[2,4,16,8,256]{4,0,3,2,1:T(2,128)(2,1)S(1)} %all_gather.9) | data formatting | bytes 1048576 | tf_op jit(solution)/shard_map/reshape | solution.py:54
  36.9 5.1 %copy.86 = bf16[2,4,16,8,8,32]{5,0,3,2,1,4:T(2,128)(2,1)} copy(bf16[2,4,16,8,8,32]{5,4,0,3,2,1:T(8,128)(2,1)} %reshape.188) | data formatting | bytes 1048576 | tf_op jit(solution)/shard_map/reshape | solution.py:54
  42.0 5.9 %reshape.215 = bf16[8,2,16384]{2,1,0:T(2,128)(2,1)} reshape(bf16[8,4,16,8,2,32]{5,4,3,2,1,0:T(2,128)(2,1)} %bitcast.86) | data formatting | bytes 1048576
  48.0 5.1 %all-to-all-start = ((bf16[8,2,16384]{2,1,0:T(2,128)(2,1)}), bf16[8,2,16384]{2,1,0:T(2,128)(2,1)S(1)}, u32[]{:S(2)}, u32[]{:S(2)}) async-start(bf16[8,2,16384]{2,1,0:T(2,128)(2,1)} %reshape.215), calls=%async_computation | async-start | bytes 1048576 | tf_op jit(solution)/shard_map/all_to_all | solution.py:56
  53.1 0.2 all-gather.5.cloned.1.call-start
  53.4 0.1 add.90
  53.5 14.7 %all-to-all-done = bf16[8,2,16384]{2,1,0:T(2,128)(2,1)S(1)} async-done(((bf16[8,2,16384]{2,1,0:T(2,128)(2,1)}), bf16[8,2,16384]{2,1,0:T(2,128)(2,1)S(1)}, u32[]{:S(2)}, u32[]{:S(2)}) %all-to-all-start) | async-done | bytes 524320 | tf_op jit(solution)/shard_map/all_to_all | solution.py:56
  68.2 2.0 %reshape.216 = bf16[8,4,16,8,2,32]{5,4,3,2,1,0:T(2,128)(2,1)} reshape(bf16[8,2,16384]{2,1,0:T(2,128)(2,1)S(1)} %all-to-all-done) | data formatting | bytes 1048576
  70.2 5.2 %copy.55 = bf16[8,2,4,16,8,32]{5,1,0,4,3,2:T(2,128)(2,1)} copy(bf16[8,2,4,16,8,32]{5,1,4,3,2,0:T(2,128)(2,1)} %bitcast.84) | data formatting | bytes 1048576 | tf_op jit(solution)/shard_map/all_to_all | solution.py:56
  75.4 1.4 slice.57
  76.8 0.5 copy.63
  77.4 2.3 %concatenate.61 = bf16[4,2,2,2,16,8,32]{6,2,1,0,5,4,3:T(2,128)(2,1)} pad(bf16[4,1,2,2,16,8,32]{6,2,1,0,5,4,3:T(2,128)(2,1)S(1)} %copy.63, bf16[]{:T(256)} %constant.72.clone.1), padding=0_0x1_0x0_0x0_0x0_0x0_0x0_0 | pad | bytes 393218 | tf_op jit(solution)/shard_map/concatenate | solution.py:60
  79.6 10.0 %all-gather.3.cloned.1.call-done = bf16[16,4,16,8,128]{4,3,2,1,0:T(8,128)(2,1)} async-done(((bf16[2,4,16,8,128]{4,3,2,1,0:T(8,128)(2,1)}), bf16[16,4,16,8,128]{4,3,2,1,0:T(8,128)(2,1)}) %all-gather.3.cloned.1.call-update) | async-done | bytes 2097168 | tf_op jit(solution)/shard_map/all_gather | solution.py:63
  89.6 16.9 %fusion.7 = bf16[3,3,3,32,128]{4,3,2,1,0:T(8,128)(2,1)} fusion(bf16[16,4,16,8,128]{4,3,2,1,0:T(8,128)(2,1)} %all-gather.3.cloned.1.call-done, bf16[16,4,16,8,32]{4,0,3,2,1:T(8,128)(2,1)} %bitcast.87, bf16[16,2,16,8,32]{4,0,3,2,1:T(8,128)(2,1)} %bitcast.90), kind=kOutput, calls=%fused_computation.12 | convolution fusion | flops 1593421824 | bytes 3104768 | tf_op jit(solution)/shard_map/conv_general_dilated | solution.py:37
  106.6 0.2 convolution_bitcast_fusion
  106.8 0.6 collective-permute-start.5
  107.4 7.5 %fusion.19 = f32[2,6,16,8,256]{4,0,3,2,1:T(2,128)S(1)} fusion(bf16[3,3,3,256,128]{4,3,2,1,0:T(8,128)(2,1)S(1)} %bitcast.83, bf16[2,4,16,8,128]{4,3,2,1,0:T(8,128)(2,1)S(1)} %bitcast.92), kind=kOutput, calls=%fused_computation.28 | convolution fusion | flops 1591738368 | bytes 3604480 | tf_op jit(solution)/shard_map/conv_general_dilated | solution.py:37
  114.9 1.1 copy-done.1
  116.1 1.0 slice.60
  117.1 1.3 collective-permute-start.8
  118.4 0.2 fusion.33
  118.6 1.6 collective-permute-start.6
  120.1 3.6 %psum.7 = bf16[1024,16]{0,1:T(8,128)(2,1)S(1)} all-reduce(f32[1024,16]{0,1:T(8,128)S(1)} %fusion.33), channel_id=1, replica_groups=mesh['groups'=2,'cam'=4,'tm'=2,'chan'=2] {'chan'}, use_global_device_ids=true, to_apply=%region_4.5 | all-reduce | flops 16384 | bytes 98304 | tf_op jit(solution)/shard_map/psum | solution.py:109
  123.7 0.2 copy.51
  123.9 0.2 reshape.186
  124.1 0.6 collective-permute-start.1
  124.7 1.9 %collective-permute-start.7 = (f32[4,128,16]{1,2,0:T(8,128)S(1)}, f32[4,128,16]{1,2,0:T(8,128)S(1)}, u32[]{:S(2)}, u32[]{:S(2)}) collective-permute-start(f32[4,128,16]{1,2,0:T(8,128)S(1)} %maximum_select_fusion.1), channel_id=1, source_target_pairs={{0,8},{4,12},{8,0},{12,4},{1,9},{5,13},{9,1},{13,5},{2,10},{6,14},... | collective-permute-start | bytes 98312 | tf_op jit(solution)/shard_map/ppermute | solution.py:25
  126.6 2.6 %collective-permute-done.1 = bf16[2,4,16,128]{3,2,1,0:T(8,128)(2,1)S(1)} collective-permute-done((bf16[2,4,16,128]{3,2,1,0:T(8,128)(2,1)S(1)}, bf16[2,4,16,128]{3,2,1,0:T(8,128)(2,1)S(1)}, u32[]{:S(2)}, u32[]{:S(2)}) %collective-permute-start.1) | collective-permute-done | bytes 32800 | tf_op jit(solution)/shard_map/ppermute | solution.py:77
  129.3 0.6 gather_fusion
  129.9 0.3 concatenate.56
  130.2 1.6 slice.58
  131.9 0.6 fusion.23
  132.5 1.9 %collective-permute-done.2 = bf16[4,4,16,128]{3,2,1,0:T(8,128)(2,1)S(1)} collective-permute-done((bf16[4,4,16,128]{3,2,1,0:T(8,128)(2,1)S(1)}, bf16[4,4,16,128]{3,2,1,0:T(8,128)(2,1)S(1)}, u32[]{:S(2)}, u32[]{:S(2)}) %collective-permute-start.2) | collective-permute-done | bytes 65568 | tf_op jit(solution)/shard_map/ppermute | solution.py:77
  134.5 1.4 fusion.13
  135.9 0.2 constant_dynamic-slice_fusion
  136.1 0.1 collective-permute-start.9
  136.1 0.1 pad_maximum_fusion.2
  136.2 0.9 fusion.28
  137.1 0.5 collective-permute-done.9
  137.7 0.3 add_convert_fusion
  137.9 0.7 copy.60
  138.7 13.8 %all-gather.5.cloned.1.call-done = bf16[3,3,3,256,128]{4,3,2,1,0:T(8,128)(2,1)} async-done(((bf16[3,3,3,32,128]{4,3,2,1,0:T(8,128)(2,1)}), bf16[3,3,3,256,128]{4,3,2,1,0:T(8,128)(2,1)}) %all-gather.5.cloned.1.call-update) | async-done | bytes 1769488 | tf_op jit(solution)/shard_map/all_gather | solution.py:66
  152.5 2.9 %copy.89 = bf16[27,256,128]{2,1,0:T(8,128)(2,1)} copy(bf16[27,256,128]{2,1,0:T(8,128)(2,1)} %bitcast.88) | data formatting | bytes 3538944
  (30 shorter events, 0.4 us)
Async XLA Ops:
  7.2 19.5 %copy-start = (bf16[27,256,128]{2,1,0:T(8,128)(2,1)S(1)}, bf16[27,256,128]{2,1,0:T(8,128)(2,1)}, u32[]{:S(2)}) copy-start(bf16[27,256,128]{2,1,0:T(8,128)(2,1)} %param.10) | copy-start | bytes 5308420
  7.2 82.4 %all-gather.3.cloned.1.call-start = ((), (), s32[]{:S(2)}) async-start(), calls=%async_computation.1 | async-start | bytes 2359296 | tf_op jit(solution)/shard_map/all_gather | solution.py:63
  11.1 15.6 %collective-permute-start = (bf16[2,2,16,8,256]{4,0,3,2,1:T(2,128)(2,1)S(1)}, bf16[2,2,16,8,256]{4,0,3,2,1:T(2,128)(2,1)S(1)}, u32[]{:S(2)}, u32[]{:S(2)}) collective-permute-start(bf16[2,2,16,8,256]{4,0,3,2,1:T(2,128)(2,1)S(1)} %slice.56), channel_id=1, source_target_pairs={{0,2},{1,3},{4,6},{5,7},{8,10},{9,11},{12,14},{13,15},{16,18},{17,... | collective-permute-start | bytes 786440 | tf_op jit(solution)/shard_map/ppermute | solution.py:13
  15.8 4.0 %collective-permute-start.3 = (bf16[1,4,16,128]{3,2,1,0:T(8,128)(2,1)}, bf16[1,4,16,128]{3,2,1,0:T(8,128)(2,1)S(1)}, u32[]{:S(2)}, u32[]{:S(2)}) collective-permute-start(bf16[1,4,16,128]{3,2,1,0:T(8,128)(2,1)} %param.15), channel_id=1, source_target_pairs={{0,4},{4,0},{8,12},{12,8},{1,5},{5,1},{9,13},{13,9},{2,6},{6,2},{1... | collective-permute-start | bytes 49160 | tf_op jit(solution)/shard_map/ppermute | solution.py:77
  20.6 4.8 %collective-permute-start.4 = (bf16[2,4,16,128]{3,2,1,0:T(8,128)(2,1)S(1)}, bf16[2,4,16,128]{3,2,1,0:T(8,128)(2,1)S(1)}, u32[]{:S(2)}, u32[]{:S(2)}) collective-permute-start(bf16[2,4,16,128]{3,2,1,0:T(8,128)(2,1)S(1)} %pad_maximum_fusion.5), channel_id=1, source_target_pairs={{0,8},{4,12},{8,0},{12,4},{1,9},{5,13},{9,1},{13,5},{2,10},{6,14},... | collective-permute-start | bytes 98312 | tf_op jit(solution)/shard_map/ppermute | solution.py:77
  33.2 0.7 copy-start.3
  48.0 20.2 %all-to-all-start = ((bf16[8,2,16384]{2,1,0:T(2,128)(2,1)}), bf16[8,2,16384]{2,1,0:T(2,128)(2,1)S(1)}, u32[]{:S(2)}, u32[]{:S(2)}) async-start(bf16[8,2,16384]{2,1,0:T(2,128)(2,1)} %reshape.215), calls=%async_computation | async-start | bytes 1048576 | tf_op jit(solution)/shard_map/all_to_all | solution.py:56
  53.1 99.4 %all-gather.5.cloned.1.call-start = ((), (), s32[]{:S(2)}) async-start(), calls=%async_computation.2 | async-start | bytes 1990656 | tf_op jit(solution)/shard_map/all_gather | solution.py:66
  89.6 17.8 %copy-start.2 = (bf16[1024,128]{1,0:T(8,128)(2,1)S(1)}, bf16[1024,128]{1,0:T(8,128)(2,1)}, u32[]{:S(2)}) copy-start(bf16[1024,128]{1,0:T(8,128)(2,1)} %fusion.6) | copy-start | bytes 786436
  106.8 11.7 %collective-permute-start.5 = (f32[1,128,16]{1,2,0:T(8,128)S(1)}, f32[1,128,16]{1,2,0:T(8,128)S(1)}, u32[]{:S(2)}, u32[]{:S(2)}) collective-permute-start(f32[1,128,16]{1,2,0:T(8,128)S(1)} %convolution_bitcast_fusion), channel_id=1, source_target_pairs={{0,2},{2,0},{1,3},{3,1},{4,6},{6,4},{5,7},{7,5},{8,10},{10,8},{9,1... | collective-permute-start | bytes 24584 | tf_op jit(solution)/shard_map/ppermute | solution.py:25
  114.9 1.1 copy-start.1
  117.1 17.4 %collective-permute-start.8 = (f32[2,2,16,8,256]{4,0,3,2,1:T(2,128)}, f32[2,2,16,8,256]{4,0,3,2,1:T(2,128)S(1)}, u32[]{:S(2)}, u32[]{:S(2)}) collective-permute-start(f32[2,2,16,8,256]{4,0,3,2,1:T(2,128)} %slice.60), channel_id=1, source_target_pairs={{2,0},{3,1},{6,4},{7,5},{10,8},{11,9},{14,12},{15,13},{18,16},{19,... | collective-permute-start | bytes 1572872 | tf_op jit(solution)/shard_map/ppermute | solution.py:13
  118.6 6.1 %collective-permute-start.6 = (f32[2,128,16]{1,2,0:T(8,128)S(1)}, f32[2,128,16]{1,2,0:T(8,128)S(1)}, u32[]{:S(2)}, u32[]{:S(2)}) collective-permute-start(f32[2,128,16]{1,2,0:T(8,128)S(1)} %maximum_select_fusion.2), channel_id=1, source_target_pairs={{0,4},{4,0},{8,12},{12,8},{1,5},{5,1},{9,13},{13,9},{2,6},{6,2},{1... | collective-permute-start | bytes 49160 | tf_op jit(solution)/shard_map/ppermute | solution.py:25
  124.1 5.1 %collective-permute-start.1 = (bf16[2,4,16,128]{3,2,1,0:T(8,128)(2,1)S(1)}, bf16[2,4,16,128]{3,2,1,0:T(8,128)(2,1)S(1)}, u32[]{:S(2)}, u32[]{:S(2)}) collective-permute-start(bf16[2,4,16,128]{3,2,1,0:T(8,128)(2,1)S(1)} %reshape.186), channel_id=1, source_target_pairs={{0,4},{4,0},{8,12},{12,8},{1,5},{5,1},{9,13},{13,9},{2,6},{6,2},{1... | collective-permute-start | bytes 98312 | tf_op jit(solution)/shard_map/ppermute | solution.py:77
  124.7 7.2 %collective-permute-start.7 = (f32[4,128,16]{1,2,0:T(8,128)S(1)}, f32[4,128,16]{1,2,0:T(8,128)S(1)}, u32[]{:S(2)}, u32[]{:S(2)}) collective-permute-start(f32[4,128,16]{1,2,0:T(8,128)S(1)} %maximum_select_fusion.1), channel_id=1, source_target_pairs={{0,8},{4,12},{8,0},{12,4},{1,9},{5,13},{9,1},{13,5},{2,10},{6,14},... | collective-permute-start | bytes 98312 | tf_op jit(solution)/shard_map/ppermute | solution.py:25
  129.2 5.2 %collective-permute-start.2 = (bf16[4,4,16,128]{3,2,1,0:T(8,128)(2,1)S(1)}, bf16[4,4,16,128]{3,2,1,0:T(8,128)(2,1)S(1)}, u32[]{:S(2)}, u32[]{:S(2)}) collective-permute-start(bf16[4,4,16,128]{3,2,1,0:T(8,128)(2,1)S(1)} %pad_maximum_fusion.3), channel_id=1, source_target_pairs={{0,8},{4,12},{8,0},{12,4},{1,9},{5,13},{9,1},{13,5},{2,10},{6,14},... | collective-permute-start | bytes 196616 | tf_op jit(solution)/shard_map/ppermute | solution.py:77
  136.1 1.6 collective-permute-start.9
Sparse Core Ops, SparseCore 0:
  35.0 54.5 all-gather.2
  106.7 45.7 all-gather.4

commit v2 on v1

--- a/solution.py
+++ b/solution.py
@@ -77,6 +77,17 @@
         blocks = jnp.concatenate([blocks, lax.ppermute(blocks, axis, pairs)], axis=0)
         step *= 2
     return blocks, lax.axis_index(axis) ^ jnp.arange(size)
+
+
+def xor_direct(block, axis):
+    size = lax.axis_size(axis)
+    if size & (size - 1):
+        return lax.all_gather(block, axis, axis=0, tiled=True), jnp.arange(size)
+    blocks = [block]
+    for partner in range(1, size):
+        pairs = [(i, i ^ partner) for i in range(size)]
+        blocks.append(lax.ppermute(block, axis, pairs))
+    return jnp.concatenate(blocks, axis=0), lax.axis_index(axis) ^ jnp.arange(size)
 
 
 def joining_matrix(rig_sizes, camera_order, owner_slot):
@@ -122,7 +133,7 @@
     )
     robot_latent = added.reshape(1, frames, height, width * lat_width)
     my_cols = lax.dynamic_slice_in_dim(mixing, cam_index * cam_dev, cam_dev, 1)
-    block_in, source = xor_gathered(cotangent, "cam")
+    block_in, source = xor_direct(cotangent, "cam")
     flat_in = block_in.reshape(block_in.shape[0], -1).astype(jnp.float32)
     rows_per = cotangent.shape[0]
     places = (source[:, None] * rows_per + jnp.arange(rows_per)[None, :]).reshape(-1)

time: 163 us -> 163 us (level)
  starting transfers between devices: 20.4 us -> 22.4 us
    ppermute x0 -> x3, starting transfers between devices: none -> 5.76 us  [xor_direct(): blocks.append(lax.ppermute(block, axis, pairs))]
    ppermute x4 -> x2, starting transfers between devices: 4.91 us -> 0.68 us  [xor_gathered(): lax.ppermute(blocks, axis, pairs)]
    all_to_all x1, starting transfers between devices: 5.12 us -> 6.79 us  [weight_grad_sliced(): mine = lax.all_to_all(chunks, axes, 0, 0, tiled=True)]
    ppermute x4 -> x2, waiting for transfers between devices: 6.07 us -> 4.49 us  [xor_gathered(): lax.ppermute(blocks, axis, pairs)]
  transfers between devices with their start and end apart: 13 -> 14, of which waited for: 7 -> 7; matrix products, arithmetic and copies ran while one was open for 28% -> 29% of each run, Pallas kernels for 0% -> 0%
where the time goes in v2:
time: 163 us; the launch traced here: 162 us
  waiting for transfers between devices  44.1 us (27%)
  local copies, waits for them, and re-layouts  36.1 us (22%)
  matrix products  33.5 us (21%)
  starting transfers between devices  22.4 us (14%)
  between operations  14.4 us (9%)
  other arithmetic  5.94 us (4%)
  blocking collectives  5.79 us (4%)
    conv_general_dilated x3, matrix products, conv3d(): lax.conv_general_dilated(lhs, rhs, window_strides=(1, 1, 1), padding=padd...  31 us
    all_to_all x1, waiting for transfers between devices, weight_grad_sliced(): mine = lax.all_to_all(chunks, axes, 0, 0, tiled=True)  15.1 us
    unnamed x16, local copies, waits for them, and re-layouts  14.8 us
    all_gather x1, waiting for transfers between devices, weight_grad_sliced(): return lax.all_gather(part, axes, axis=3, tiled=True)  13.8 us
    all_gather x1, waiting for transfers between devices, weight_grad_sliced(): dpre_all = lax.all_gather(dpre5, axes, axis=0, tiled=True)  8.67 us
    reshape x2, local copies, waits for them, and re-layouts, weight_grad_sliced(): chunks = whole_now.reshape(cam_dev, frames, height, width, count, piece)  7.17 us
    all_to_all x1, starting transfers between devices, weight_grad_sliced(): mine = lax.all_to_all(chunks, axes, 0, 0, tiled=True)  6.79 us
    ppermute x3, starting transfers between devices, xor_direct(): blocks.append(lax.ppermute(block, axis, pairs))  5.76 us
  transfers between devices with their start and end apart: 14, of which 7 were waited for; matrix products, arithmetic and copies ran while one was open for 29% of the time, Pallas kernels for 0%

profile of v2, /device:TPU:0, one launch (start us, length us, event | category | flops | bytes accessed | tf_op | source)
XLA Modules:
  0.0 162.3 jit_solution(1481228000118063600)
XLA Ops:
  7.2 5.1 %collective-permute-start.5 = (bf16[1,4,16,128]{3,2,1,0:T(8,128)(2,1)}, bf16[1,4,16,128]{3,2,1,0:T(8,128)(2,1)S(1)}, u32[]{:S(2)}, u32[]{:S(2)}) collective-permute-start(bf16[1,4,16,128]{3,2,1,0:T(8,128)(2,1)} %param.15), channel_id=1, source_target_pairs={{0,12},{4,8},{8,4},{12,0},{1,13},{5,9},{9,5},{13,1},{2,14},{6,10},... | collective-permute-start | bytes 49160 | tf_op jit(solution)/shard_map/ppermute | solution.py:89
  12.3 0.6 collective-permute-start.3
  13.0 1.2 copy.49
  14.2 2.2 %all_gather.9 = bf16[2,4,16,8,256]{4,0,3,2,1:T(2,128)(2,1)S(1)} all-gather(bf16[2,4,16,8,128]{4,0,3,2,1:T(2,128)(2,1)S(1)} %copy.49), channel_id=1, replica_groups=mesh['groups'=2,'cam'=4,'tm'=2,'chan'=2] {'chan'}, dimensions={4}, use_global_device_ids=true | all-gather | bytes 786432 | tf_op jit(solution)/shard_map/all_gather | solution.py:110
  16.4 0.2 slice.56
  16.6 3.6 %collective-permute-start = (bf16[2,2,16,8,256]{4,0,3,2,1:T(2,128)(2,1)S(1)}, bf16[2,2,16,8,256]{4,0,3,2,1:T(2,128)(2,1)S(1)}, u32[]{:S(2)}, u32[]{:S(2)}) collective-permute-start(bf16[2,2,16,8,256]{4,0,3,2,1:T(2,128)(2,1)S(1)} %slice.56), channel_id=1, source_target_pairs={{0,2},{1,3},{4,6},{5,7},{8,10},{9,11},{12,14},{13,15},{16,18},{17,... | collective-permute-start | bytes 786440 | tf_op jit(solution)/shard_map/ppermute | solution.py:13
  20.1 0.8 reduce-window.8
  21.0 0.7 convert_reduce_fusion
  21.7 0.8 select_reduce_fusion.1
  22.5 0.1 constant_dynamic-slice_fusion.1
  22.6 0.6 gather_fusion.1
  23.2 0.7 pad_maximum_fusion.4
  23.9 0.3 convolution_convert_fusion
  24.2 0.2 reshape.191
  24.5 1.6 collective-permute-done
  26.0 6.6 %fusion.12 = f32[2,4,16,8,128]{4,0,3,2,1:T(2,128)S(1)} fusion(bf16[3,3,3,256,128]{4,3,2,1,0:T(8,128)(2,1)S(1)} %bitcast.82, bf16[2,4,16,8,256]{4,0,3,2,1:T(2,128)(2,1)S(1)} %all_gather.9, bf16[2,2,16,8,256]{4,0,3,2,1:T(2,128)(2,1)S(1)} %collective-permute-done), kind=kOutput, calls=%fused_computation.15 | convolution fusion | flops 1593311232 | bytes 3080192 | tf_op jit(solution)/shard_map/conv_general_dilated | solution.py:37
  32.6 0.2 multiply_convert_fusion
  32.8 0.2 fusion.16
  33.0 0.3 copy-done.3
  33.3 0.9 fusion.6
  34.2 2.0 %reshape.188 = bf16[2,4,16,8,8,32]{5,4,0,3,2,1:T(8,128)(2,1)} reshape(bf16[2,4,16,8,256]{4,0,3,2,1:T(2,128)(2,1)S(1)} %all_gather.9) | data formatting | bytes 1048576 | tf_op jit(solution)/shard_map/reshape | solution.py:54
  36.2 5.1 %copy.86 = bf16[2,4,16,8,8,32]{5,0,3,2,1,4:T(2,128)(2,1)} copy(bf16[2,4,16,8,8,32]{5,4,0,3,2,1:T(8,128)(2,1)} %reshape.188) | data formatting | bytes 1048576 | tf_op jit(solution)/shard_map/reshape | solution.py:54
  41.4 5.9 %reshape.215 = bf16[8,2,16384]{2,1,0:T(2,128)(2,1)} reshape(bf16[8,4,16,8,2,32]{5,4,3,2,1,0:T(2,128)(2,1)} %bitcast.86) | data formatting | bytes 1048576
  47.3 6.8 %all-to-all-start = ((bf16[8,2,16384]{2,1,0:T(2,128)(2,1)}), bf16[8,2,16384]{2,1,0:T(2,128)(2,1)S(1)}, u32[]{:S(2)}, u32[]{:S(2)}) async-start(bf16[8,2,16384]{2,1,0:T(2,128)(2,1)} %reshape.215), calls=%async_computation | async-start | bytes 1048576 | tf_op jit(solution)/shard_map/all_to_all | solution.py:56
  54.1 0.2 all-gather.5.cloned.1.call-start
  54.3 0.1 iota_add_fusion
  54.4 0.1 add.90
  54.5 15.1 %all-to-all-done = bf16[8,2,16384]{2,1,0:T(2,128)(2,1)S(1)} async-done(((bf16[8,2,16384]{2,1,0:T(2,128)(2,1)}), bf16[8,2,16384]{2,1,0:T(2,128)(2,1)S(1)}, u32[]{:S(2)}, u32[]{:S(2)}) %all-to-all-start) | async-done | bytes 524320 | tf_op jit(solution)/shard_map/all_to_all | solution.py:56
  69.5 2.0 %reshape.216 = bf16[8,4,16,8,2,32]{5,4,3,2,1,0:T(2,128)(2,1)} reshape(bf16[8,2,16384]{2,1,0:T(2,128)(2,1)S(1)} %all-to-all-done) | data formatting | bytes 1048576
  71.6 5.2 %copy.55 = bf16[8,2,4,16,8,32]{5,1,0,4,3,2:T(2,128)(2,1)} copy(bf16[8,2,4,16,8,32]{5,1,4,3,2,0:T(2,128)(2,1)} %bitcast.84) | data formatting | bytes 1048576 | tf_op jit(solution)/shard_map/all_to_all | solution.py:56
  76.8 1.4 slice.57
  78.2 0.5 copy.63
  78.8 2.3 %concatenate.57 = bf16[4,2,2,2,16,8,32]{6,2,1,0,5,4,3:T(2,128)(2,1)} pad(bf16[4,1,2,2,16,8,32]{6,2,1,0,5,4,3:T(2,128)(2,1)S(1)} %copy.63, bf16[]{:T(256)} %constant.72.clone.1), padding=0_0x1_0x0_0x0_0x0_0x0_0x0_0 | pad | bytes 393218 | tf_op jit(solution)/shard_map/concatenate | solution.py:60
  81.0 8.7 %all-gather.3.cloned.1.call-done = bf16[16,4,16,8,128]{4,3,2,1,0:T(8,128)(2,1)} async-done(((bf16[2,4,16,8,128]{4,3,2,1,0:T(8,128)(2,1)}), bf16[16,4,16,8,128]{4,3,2,1,0:T(8,128)(2,1)}) %all-gather.3.cloned.1.call-update) | async-done | bytes 2097168 | tf_op jit(solution)/shard_map/all_gather | solution.py:63
  89.7 16.9 %fusion.7 = bf16[3,3,3,32,128]{4,3,2,1,0:T(8,128)(2,1)} fusion(bf16[16,4,16,8,128]{4,3,2,1,0:T(8,128)(2,1)} %all-gather.3.cloned.1.call-done, bf16[16,4,16,8,32]{4,0,3,2,1:T(8,128)(2,1)} %bitcast.87, bf16[16,2,16,8,32]{4,0,3,2,1:T(8,128)(2,1)} %bitcast.90), kind=kOutput, calls=%fused_computation.12 | convolution fusion | flops 1593421824 | bytes 3104768 | tf_op jit(solution)/shard_map/conv_general_dilated | solution.py:37
  106.7 0.2 convolution_bitcast_fusion
  106.9 0.6 collective-permute-start.6
  107.5 7.5 %fusion.19 = f32[2,6,16,8,256]{4,0,3,2,1:T(2,128)S(1)} fusion(bf16[3,3,3,256,128]{4,3,2,1,0:T(8,128)(2,1)S(1)} %bitcast.83, bf16[2,4,16,8,128]{4,3,2,1,0:T(8,128)(2,1)S(1)} %bitcast.92), kind=kOutput, calls=%fused_computation.28 | convolution fusion | flops 1591738368 | bytes 3604480 | tf_op jit(solution)/shard_map/conv_general_dilated | solution.py:37
  115.0 1.1 copy-done.1
  116.1 1.0 slice.60
  117.2 1.3 collective-permute-start.9
  118.4 0.2 fusion.33
  118.6 1.6 collective-permute-start.7
  120.2 3.6 %psum.7 = bf16[1024,16]{0,1:T(8,128)(2,1)S(1)} all-reduce(f32[1024,16]{0,1:T(8,128)S(1)} %fusion.33), channel_id=1, replica_groups=mesh['groups'=2,'cam'=4,'tm'=2,'chan'=2] {'chan'}, use_global_device_ids=true, to_apply=%region_4.5 | all-reduce | flops 16384 | bytes 98304 | tf_op jit(solution)/shard_map/psum | solution.py:120
  123.8 0.2 copy.51
  124.0 0.2 reshape.186
  124.2 0.6 collective-permute-start.1
  124.8 1.9 %collective-permute-start.8 = (f32[4,128,16]{1,2,0:T(8,128)S(1)}, f32[4,128,16]{1,2,0:T(8,128)S(1)}, u32[]{:S(2)}, u32[]{:S(2)}) collective-permute-start(f32[4,128,16]{1,2,0:T(8,128)S(1)} %maximum_select_fusion.1), channel_id=1, source_target_pairs={{0,8},{4,12},{8,0},{12,4},{1,9},{5,13},{9,1},{13,5},{2,10},{6,14},... | collective-permute-start | bytes 98312 | tf_op jit(solution)/shard_map/ppermute | solution.py:25
  126.7 2.6 %collective-permute-done.1 = bf16[2,4,16,128]{3,2,1,0:T(8,128)(2,1)S(1)} collective-permute-done((bf16[2,4,16,128]{3,2,1,0:T(8,128)(2,1)S(1)}, bf16[2,4,16,128]{3,2,1,0:T(8,128)(2,1)S(1)}, u32[]{:S(2)}, u32[]{:S(2)}) %collective-permute-start.1) | collective-permute-done | bytes 32800 | tf_op jit(solution)/shard_map/ppermute | solution.py:77
  129.4 0.6 gather_fusion
  130.0 0.3 concatenate.52
  130.3 1.6 slice.58
  132.0 0.6 fusion.23
  132.6 1.9 %collective-permute-done.2 = bf16[4,4,16,128]{3,2,1,0:T(8,128)(2,1)S(1)} collective-permute-done((bf16[4,4,16,128]{3,2,1,0:T(8,128)(2,1)S(1)}, bf16[4,4,16,128]{3,2,1,0:T(8,128)(2,1)S(1)}, u32[]{:S(2)}, u32[]{:S(2)}) %collective-permute-start.2) | collective-permute-done | bytes 65568 | tf_op jit(solution)/shard_map/ppermute | solution.py:77
  134.6 1.4 fusion.13
  135.9 0.2 constant_dynamic-slice_fusion
  136.1 0.1 collective-permute-start.10
  136.2 0.1 pad_maximum_fusion.2
  136.3 0.9 fusion.28
  137.2 0.5 collective-permute-done.10
  137.7 0.3 add_convert_fusion
  138.0 0.7 copy.60
  138.8 13.8 %all-gather.5.cloned.1.call-done = bf16[3,3,3,256,128]{4,3,2,1,0:T(8,128)(2,1)} async-done(((bf16[3,3,3,32,128]{4,3,2,1,0:T(8,128)(2,1)}), bf16[3,3,3,256,128]{4,3,2,1,0:T(8,128)(2,1)}) %all-gather.5.cloned.1.call-update) | async-done | bytes 1769488 | tf_op jit(solution)/shard_map/all_gather | solution.py:66
  152.5 2.9 %copy.89 = bf16[27,256,128]{2,1,0:T(8,128)(2,1)} copy(bf16[27,256,128]{2,1,0:T(8,128)(2,1)} %bitcast.88) | data formatting | bytes 3538944
  (31 shorter events, 0.4 us)
Async XLA Ops:
  7.2 18.9 %copy-start = (bf16[27,256,128]{2,1,0:T(8,128)(2,1)S(1)}, bf16[27,256,128]{2,1,0:T(8,128)(2,1)}, u32[]{:S(2)}) copy-start(bf16[27,256,128]{2,1,0:T(8,128)(2,1)} %param.10) | copy-start | bytes 5308420
  7.2 82.5 %all-gather.3.cloned.1.call-start = ((), (), s32[]{:S(2)}) async-start(), calls=%async_computation.1 | async-start | bytes 2359296 | tf_op jit(solution)/shard_map/all_gather | solution.py:63
  7.2 15.9 %collective-permute-start.5 = (bf16[1,4,16,128]{3,2,1,0:T(8,128)(2,1)}, bf16[1,4,16,128]{3,2,1,0:T(8,128)(2,1)S(1)}, u32[]{:S(2)}, u32[]{:S(2)}) collective-permute-start(bf16[1,4,16,128]{3,2,1,0:T(8,128)(2,1)} %param.15), channel_id=1, source_target_pairs={{0,12},{4,8},{8,4},{12,0},{1,13},{5,9},{9,5},{13,1},{2,14},{6,10},... | collective-permute-start | bytes 49160 | tf_op jit(solution)/shard_map/ppermute | solution.py:89
  12.3 10.8 %collective-permute-start.4 = (bf16[1,4,16,128]{3,2,1,0:T(8,128)(2,1)}, bf16[1,4,16,128]{3,2,1,0:T(8,128)(2,1)S(1)}, u32[]{:S(2)}, u32[]{:S(2)}) collective-permute-start(bf16[1,4,16,128]{3,2,1,0:T(8,128)(2,1)} %param.15), channel_id=1, source_target_pairs={{0,8},{4,12},{8,0},{12,4},{1,9},{5,13},{9,1},{13,5},{2,10},{6,14},... | collective-permute-start | bytes 49160 | tf_op jit(solution)/shard_map/ppermute | solution.py:89
  12.3 10.8 %collective-permute-start.3 = (bf16[1,4,16,128]{3,2,1,0:T(8,128)(2,1)}, bf16[1,4,16,128]{3,2,1,0:T(8,128)(2,1)S(1)}, u32[]{:S(2)}, u32[]{:S(2)}) collective-permute-start(bf16[1,4,16,128]{3,2,1,0:T(8,128)(2,1)} %param.15), channel_id=1, source_target_pairs={{0,4},{4,0},{8,12},{12,8},{1,5},{5,1},{9,13},{13,9},{2,6},{6,2},{1... | collective-permute-start | bytes 49160 | tf_op jit(solution)/shard_map/ppermute | solution.py:89
  16.6 9.4 %collective-permute-start = (bf16[2,2,16,8,256]{4,0,3,2,1:T(2,128)(2,1)S(1)}, bf16[2,2,16,8,256]{4,0,3,2,1:T(2,128)(2,1)S(1)}, u32[]{:S(2)}, u32[]{:S(2)}) collective-permute-start(bf16[2,2,16,8,256]{4,0,3,2,1:T(2,128)(2,1)S(1)} %slice.56), channel_id=1, source_target_pairs={{0,2},{1,3},{4,6},{5,7},{8,10},{9,11},{12,14},{13,15},{16,18},{17,... | collective-permute-start | bytes 786440 | tf_op jit(solution)/shard_map/ppermute | solution.py:13
  32.6 0.7 copy-start.3
  47.3 22.3 %all-to-all-start = ((bf16[8,2,16384]{2,1,0:T(2,128)(2,1)}), bf16[8,2,16384]{2,1,0:T(2,128)(2,1)S(1)}, u32[]{:S(2)}, u32[]{:S(2)}) async-start(bf16[8,2,16384]{2,1,0:T(2,128)(2,1)} %reshape.215), calls=%async_computation | async-start | bytes 1048576 | tf_op jit(solution)/shard_map/all_to_all | solution.py:56
  54.1 98.5 %all-gather.5.cloned.1.call-start = ((), (), s32[]{:S(2)}) async-start(), calls=%async_computation.2 | async-start | bytes 1990656 | tf_op jit(solution)/shard_map/all_gather | solution.py:66
  89.7 17.8 %copy-start.2 = (bf16[1024,128]{1,0:T(8,128)(2,1)S(1)}, bf16[1024,128]{1,0:T(8,128)(2,1)}, u32[]{:S(2)}) copy-start(bf16[1024,128]{1,0:T(8,128)(2,1)} %fusion.6) | copy-start | bytes 786436
  106.9 11.7 %collective-permute-start.6 = (f32[1,128,16]{1,2,0:T(8,128)S(1)}, f32[1,128,16]{1,2,0:T(8,128)S(1)}, u32[]{:S(2)}, u32[]{:S(2)}) collective-permute-start(f32[1,128,16]{1,2,0:T(8,128)S(1)} %convolution_bitcast_fusion), channel_id=1, source_target_pairs={{0,2},{2,0},{1,3},{3,1},{4,6},{6,4},{5,7},{7,5},{8,10},{10,8},{9,1... | collective-permute-start | bytes 24584 | tf_op jit(solution)/shard_map/ppermute | solution.py:25
  115.0 1.1 copy-start.1
  117.2 17.4 %collective-permute-start.9 = (f32[2,2,16,8,256]{4,0,3,2,1:T(2,128)}, f32[2,2,16,8,256]{4,0,3,2,1:T(2,128)S(1)}, u32[]{:S(2)}, u32[]{:S(2)}) collective-permute-start(f32[2,2,16,8,256]{4,0,3,2,1:T(2,128)} %slice.60), channel_id=1, source_target_pairs={{2,0},{3,1},{6,4},{7,5},{10,8},{11,9},{14,12},{15,13},{18,16},{19,... | collective-permute-start | bytes 1572872 | tf_op jit(solution)/shard_map/ppermute | solution.py:13
  118.6 6.1 %collective-permute-start.7 = (f32[2,128,16]{1,2,0:T(8,128)S(1)}, f32[2,128,16]{1,2,0:T(8,128)S(1)}, u32[]{:S(2)}, u32[]{:S(2)}) collective-permute-start(f32[2,128,16]{1,2,0:T(8,128)S(1)} %maximum_select_fusion.2), channel_id=1, source_target_pairs={{0,4},{4,0},{8,12},{12,8},{1,5},{5,1},{9,13},{13,9},{2,6},{6,2},{1... | collective-permute-start | bytes 49160 | tf_op jit(solution)/shard_map/ppermute | solution.py:25
  124.2 5.1 %collective-permute-start.1 = (bf16[2,4,16,128]{3,2,1,0:T(8,128)(2,1)S(1)}, bf16[2,4,16,128]{3,2,1,0:T(8,128)(2,1)S(1)}, u32[]{:S(2)}, u32[]{:S(2)}) collective-permute-start(bf16[2,4,16,128]{3,2,1,0:T(8,128)(2,1)S(1)} %reshape.186), channel_id=1, source_target_pairs={{0,4},{4,0},{8,12},{12,8},{1,5},{5,1},{9,13},{13,9},{2,6},{6,2},{1... | collective-permute-start | bytes 98312 | tf_op jit(solution)/shard_map/ppermute | solution.py:77
  124.8 7.2 %collective-permute-start.8 = (f32[4,128,16]{1,2,0:T(8,128)S(1)}, f32[4,128,16]{1,2,0:T(8,128)S(1)}, u32[]{:S(2)}, u32[]{:S(2)}) collective-permute-start(f32[4,128,16]{1,2,0:T(8,128)S(1)} %maximum_select_fusion.1), channel_id=1, source_target_pairs={{0,8},{4,12},{8,0},{12,4},{1,9},{5,13},{9,1},{13,5},{2,10},{6,14},... | collective-permute-start | bytes 98312 | tf_op jit(solution)/shard_map/ppermute | solution.py:25
  129.3 5.2 %collective-permute-start.2 = (bf16[4,4,16,128]{3,2,1,0:T(8,128)(2,1)S(1)}, bf16[4,4,16,128]{3,2,1,0:T(8,128)(2,1)S(1)}, u32[]{:S(2)}, u32[]{:S(2)}) collective-permute-start(bf16[4,4,16,128]{3,2,1,0:T(8,128)(2,1)S(1)} %pad_maximum_fusion.3), channel_id=1, source_target_pairs={{0,8},{4,12},{8,0},{12,4},{1,9},{5,13},{9,1},{13,5},{2,10},{6,14},... | collective-permute-start | bytes 196616 | tf_op jit(solution)/shard_map/ppermute | solution.py:77
  136.1 1.6 collective-permute-start.10
Sparse Core Ops, SparseCore 0:
  34.3 55.2 all-gather.2
  106.8 45.7 all-gather.4

commit v3 on v1

--- a/solution.py
+++ b/solution.py
@@ -61,7 +61,10 @@
     timed_all = jnp.concatenate([before, mine], axis=3)
     timed_all = timed_all.reshape(count * cam_dev, frames + KT - 1, height, width, piece)
     dpre_all = lax.all_gather(dpre5, axes, axis=0, tiled=True)
-    part = conv3d(timed_all, dpre_all, space_pad, ("CDHWN", "IDHWO", "DHWNC"))
+    padded_all = jnp.pad(timed_all, ((0, 0), (0, 0)) + tuple(space_pad[1:]) + ((0, 0),))
+    swap_pad = [(KT - 1, KT - 1), (KS - 1, KS - 1), (KS - 1, KS - 1)]
+    part = conv3d(dpre_all, padded_all, swap_pad, ("CDHWN", "IDHWO", "DHWCN"))
+    part = part[::-1, ::-1, ::-1]
     part = part.astype(jnp.bfloat16)
     return lax.all_gather(part, axes, axis=3, tiled=True)
 

time: 163 us -> 178 us (1.092)
  local copies, waits for them, and re-layouts: 36.3 us -> 54.3 us
  waiting for transfers between devices: 45.1 us -> 35.3 us
  other arithmetic: 6.66 us -> 11.2 us
    another operation x0 -> x1, local copies, waits for them, and re-layouts: none -> 23.2 us
    all_gather x1, waiting for transfers between devices: 9.97 us -> 0.01 us  [weight_grad_sliced(): dpre_all = lax.all_gather(dpre5, axes, axis=0, tiled=True)]
    concatenate x0 -> x1, other arithmetic: none -> 4.5 us  [weight_grad_sliced(): timed_all = jnp.concatenate([before, mine], axis=3)]
    ppermute x4, starting transfers between devices: 4.91 us -> 8.22 us  [xor_gathered(): lax.ppermute(blocks, axis, pairs)]
    all_to_all x1, local copies, waits for them, and re-layouts: 5.24 us -> 2.12 us  [weight_grad_sliced(): mine = lax.all_to_all(chunks, axes, 0, 0, tiled=True)]
    ppermute x3, starting transfers between devices: 4.03 us -> 1.6 us  [gathered(): other = lax.ppermute(blocks, axis, pairs)]
    all_gather x1, waiting for transfers between devices: 13.8 us -> 15.8 us  [weight_grad_sliced(): return lax.all_gather(part, axes, axis=3, tiled=True)]
    concatenate x1, local copies, waits for them, and re-layouts: 2.25 us -> 0.22 us  [weight_grad_sliced(): before = jnp.concatenate([head, tail], axis=1)]
  transfers between devices with their start and end apart: 13 -> 13, of which waited for: 7 -> 6; matrix products, arithmetic and copies ran while one was open for 28% -> 39% of each run, Pallas kernels for 0% -> 0%
where the time goes in v3:
time: 178 us; the launch traced here: 176 us
  local copies, waits for them, and re-layouts  54.3 us (31%)
  waiting for transfers between devices  35.3 us (20%)
  matrix products  34 us (19%)
  starting transfers between devices  21.3 us (12%)
  between operations  14.4 us (8%)
  other arithmetic  11.2 us (6%)
  blocking collectives  5.93 us (3%)
    conv_general_dilated x3, matrix products, conv3d(): lax.conv_general_dilated(lhs, rhs, window_strides=(1, 1, 1), padding=padd...  31.5 us
    another operation x1, local copies, waits for them, and re-layouts  23.2 us
    all_gather x1, waiting for transfers between devices, weight_grad_sliced(): return lax.all_gather(part, axes, axis=3, tiled=True)  15.8 us
    all_to_all x1, waiting for transfers between devices, weight_grad_sliced(): mine = lax.all_to_all(chunks, axes, 0, 0, tiled=True)  14.7 us
    unnamed x16, local copies, waits for them, and re-layouts  14.3 us
    ppermute x4, starting transfers between devices, xor_gathered(): lax.ppermute(blocks, axis, pairs)  8.22 us
    reshape x2, local copies, waits for them, and re-layouts, weight_grad_sliced(): chunks = whole_now.reshape(cam_dev, frames, height, width, count, piece)  7.21 us
    ppermute x2, starting transfers between devices, shifted(): return lax.ppermute(shard, axis, pairs)  6.01 us
  transfers between devices with their start and end apart: 13, of which 6 were waited for; matrix products, arithmetic and copies ran while one was open for 39% of the time, Pallas kernels for 0%

profile of v3, /device:TPU:0, one launch (start us, length us, event | category | flops | bytes accessed | tf_op | source)
XLA Modules:
  0.0 176.4 jit_solution(8260501938237082980)
XLA Ops:
  7.2 1.3 copy.61
  8.6 2.3 %all_gather.9 = bf16[2,4,16,8,256]{4,0,3,2,1:T(2,128)(2,1)S(1)} all-gather(bf16[2,4,16,8,128]{4,0,3,2,1:T(2,128)(2,1)S(1)} %copy.61), channel_id=1, replica_groups=mesh['groups'=2,'cam'=4,'tm'=2,'chan'=2] {'chan'}, dimensions={4}, use_global_device_ids=true | all-gather | bytes 786432 | tf_op jit(solution)/shard_map/all_gather | solution.py:102
  10.9 0.2 slice.56
  11.1 4.7 %collective-permute-start = (bf16[2,2,16,8,256]{4,0,3,2,1:T(2,128)(2,1)S(1)}, bf16[2,2,16,8,256]{4,0,3,2,1:T(2,128)(2,1)S(1)}, u32[]{:S(2)}, u32[]{:S(2)}) collective-permute-start(bf16[2,2,16,8,256]{4,0,3,2,1:T(2,128)(2,1)S(1)} %slice.56), channel_id=1, source_target_pairs={{0,2},{1,3},{4,6},{5,7},{8,10},{9,11},{12,14},{13,15},{16,18},{17,... | collective-permute-start | bytes 786440 | tf_op jit(solution)/shard_map/ppermute | solution.py:13
  15.8 1.6 collective-permute-start.3
  17.4 0.8 reduce-window.8
  18.3 0.7 convert_reduce_fusion
  19.0 0.8 select_reduce_fusion.1
  19.8 0.7 pad_maximum_fusion.5
  20.6 2.6 %collective-permute-start.4 = (bf16[2,4,16,128]{3,2,1,0:T(8,128)(2,1)S(1)}, bf16[2,4,16,128]{3,2,1,0:T(8,128)(2,1)S(1)}, u32[]{:S(2)}, u32[]{:S(2)}) collective-permute-start(bf16[2,4,16,128]{3,2,1,0:T(8,128)(2,1)S(1)} %pad_maximum_fusion.5), channel_id=1, source_target_pairs={{0,8},{4,12},{8,0},{12,4},{1,9},{5,13},{9,1},{13,5},{2,10},{6,14},... | collective-permute-start | bytes 98312 | tf_op jit(solution)/shard_map/ppermute | solution.py:80
  23.1 0.1 constant_dynamic-slice_fusion.1
  23.2 0.6 gather_fusion.1
  23.8 1.6 collective-permute-done.4
  25.4 0.7 pad_maximum_fusion.4
  26.1 0.3 convolution_convert_fusion
  26.4 0.2 reshape.191
  26.7 6.6 %fusion.13 = f32[2,4,16,8,128]{4,0,3,2,1:T(2,128)S(1)} fusion(bf16[3,3,3,256,128]{4,3,2,1,0:T(8,128)(2,1)S(1)} %bitcast.82, bf16[2,4,16,8,256]{4,0,3,2,1:T(2,128)(2,1)S(1)} %all_gather.9, bf16[2,2,16,8,256]{4,0,3,2,1:T(2,128)(2,1)S(1)} %collective-permute-done), kind=kOutput, calls=%fused_computation.24 | convolution fusion | flops 1593311232 | bytes 3080192 | tf_op jit(solution)/shard_map/conv_general_dilated | solution.py:37
  33.2 0.2 multiply_convert_fusion
  33.4 0.2 fusion.17
  33.6 0.9 fusion.12
  34.6 2.1 %reshape.188 = bf16[2,4,16,8,8,32]{5,4,0,3,2,1:T(8,128)(2,1)} reshape(bf16[2,4,16,8,256]{4,0,3,2,1:T(2,128)(2,1)S(1)} %all_gather.9) | data formatting | bytes 1048576 | tf_op jit(solution)/shard_map/reshape | solution.py:54
  36.7 5.1 %copy.99 = bf16[2,4,16,8,8,32]{5,0,3,2,1,4:T(2,128)(2,1)} copy(bf16[2,4,16,8,8,32]{5,4,0,3,2,1:T(8,128)(2,1)} %reshape.188) | data formatting | bytes 1048576 | tf_op jit(solution)/shard_map/reshape | solution.py:54
  41.8 5.9 %reshape.215 = bf16[8,2,16384]{2,1,0:T(2,128)(2,1)} reshape(bf16[8,4,16,8,2,32]{5,4,3,2,1,0:T(2,128)(2,1)} %bitcast.87) | data formatting | bytes 1048576
  47.7 5.1 %all-to-all-start = ((bf16[8,2,16384]{2,1,0:T(2,128)(2,1)}), bf16[8,2,16384]{2,1,0:T(2,128)(2,1)S(1)}, u32[]{:S(2)}, u32[]{:S(2)}) async-start(bf16[8,2,16384]{2,1,0:T(2,128)(2,1)} %reshape.215), calls=%async_computation | async-start | bytes 1048576 | tf_op jit(solution)/shard_map/all_to_all | solution.py:56
  52.8 0.2 all-gather.5.cloned.1.call-start
  53.1 0.1 add.92
  53.2 14.7 %all-to-all-done = bf16[8,2,16384]{2,1,0:T(2,128)(2,1)S(1)} async-done(((bf16[8,2,16384]{2,1,0:T(2,128)(2,1)}), bf16[8,2,16384]{2,1,0:T(2,128)(2,1)S(1)}, u32[]{:S(2)}, u32[]{:S(2)}) %all-to-all-start) | async-done | bytes 524320 | tf_op jit(solution)/shard_map/all_to_all | solution.py:56
  67.9 2.0 %reshape.216 = bf16[8,4,16,8,2,32]{5,4,3,2,1,0:T(2,128)(2,1)} reshape(bf16[8,2,16384]{2,1,0:T(2,128)(2,1)S(1)} %all-to-all-done) | data formatting | bytes 1048576
  69.9 2.1 %copy.67 = bf16[8,2,4,16,8,32]{5,4,3,2,1,0:T(8,128)(2,1)S(1)} copy(bf16[8,2,4,16,8,32]{5,1,4,3,2,0:T(2,128)(2,1)} %bitcast.84) | data formatting | bytes 1048576 | tf_op jit(solution)/shard_map/all_to_all | solution.py:56
  72.1 1.4 slice.57
  73.5 0.1 copy.76
  73.6 0.2 concatenate.61
  73.8 4.5 %fusion.6 = bf16[16,6,18,10,32]{4,3,2,1,0:T(8,128)(2,1)} fusion(bf16[16,4,16,8,32]{4,3,2,1,0:T(8,128)(2,1)S(1)} %bitcast.86, bf16[16,2,16,8,32]{4,3,2,1,0:T(8,128)(2,1)S(1)} %bitcast.88), kind=kLoop, calls=%fused_computation.13 | loop fusion | flops 8294400 | bytes 1892352 | tf_op jit(solution)/shard_map/concatenate | solution.py:61
  78.3 23.2 %reverse.3 = bf16[16,6,18,10,32]{4,3,2,1,0:T(8,128)(2,1)} reverse(bf16[16,6,18,10,32]{4,3,2,1,0:T(8,128)(2,1)} %fusion.6), dimensions={1,2,3} | reverse | bytes 2211840 | tf_op jit(solution)/shard_map/reverse
  101.5 17.5 %fusion.8 = bf16[3,3,3,32,128]{4,3,2,1,0:T(8,128)(2,1)S(1)} fusion(bf16[16,6,18,10,32]{4,3,2,1,0:T(8,128)(2,1)} %reverse.3, bf16[16,4,16,8,128]{4,3,2,1,0:T(8,128)(2,1)} %all-gather.3.cloned.1.call-done), kind=kOutput, calls=%fused_computation.15 | convolution fusion | flops 1811939328 | bytes 3424256 | tf_op jit(solution)/shard_map/conv_general_dilated | solution.py:37
  118.9 0.7 rev.6
  119.7 0.2 convolution_bitcast_fusion
  119.9 1.1 collective-permute-start.5
  121.1 7.5 %fusion.20 = f32[2,6,16,8,256]{4,0,3,2,1:T(2,128)S(1)} fusion(bf16[3,3,3,256,128]{4,3,2,1,0:T(8,128)(2,1)S(1)} %bitcast.83, bf16[2,4,16,8,128]{4,3,2,1,0:T(8,128)(2,1)S(1)} %bitcast.92), kind=kOutput, calls=%fused_computation.38 | convolution fusion | flops 1591738368 | bytes 3604480 | tf_op jit(solution)/shard_map/conv_general_dilated | solution.py:37
  128.6 1.1 copy-done.1
  129.7 1.0 slice.60
  130.7 1.3 collective-permute-start.8
  132.0 0.2 fusion.33
  132.3 3.6 %psum.7 = bf16[1024,16]{0,1:T(8,128)(2,1)S(1)} all-reduce(f32[1024,16]{0,1:T(8,128)S(1)} %fusion.33), channel_id=1, replica_groups=mesh['groups'=2,'cam'=4,'tm'=2,'chan'=2] {'chan'}, use_global_device_ids=true, to_apply=%region_4.5 | all-reduce | flops 16384 | bytes 98304 | tf_op jit(solution)/shard_map/psum | solution.py:112
  135.9 0.2 copy.63
  136.1 0.2 reshape.186
  136.3 2.1 %collective-permute-start.1 = (bf16[2,4,16,128]{3,2,1,0:T(8,128)(2,1)S(1)}, bf16[2,4,16,128]{3,2,1,0:T(8,128)(2,1)S(1)}, u32[]{:S(2)}, u32[]{:S(2)}) collective-permute-start(bf16[2,4,16,128]{3,2,1,0:T(8,128)(2,1)S(1)} %reshape.186), channel_id=1, source_target_pairs={{0,4},{4,0},{8,12},{12,8},{1,5},{5,1},{9,13},{13,9},{2,6},{6,2},{1... | collective-permute-start | bytes 98312 | tf_op jit(solution)/shard_map/ppermute | solution.py:80
  138.4 0.4 collective-permute-start.7
  138.8 2.4 %collective-permute-done.1 = bf16[2,4,16,128]{3,2,1,0:T(8,128)(2,1)S(1)} collective-permute-done((bf16[2,4,16,128]{3,2,1,0:T(8,128)(2,1)S(1)}, bf16[2,4,16,128]{3,2,1,0:T(8,128)(2,1)S(1)}, u32[]{:S(2)}, u32[]{:S(2)}) %collective-permute-start.1) | collective-permute-done | bytes 32800 | tf_op jit(solution)/shard_map/ppermute | solution.py:80
  141.2 1.9 %collective-permute-start.2 = (bf16[4,4,16,128]{3,2,1,0:T(8,128)(2,1)S(1)}, bf16[4,4,16,128]{3,2,1,0:T(8,128)(2,1)S(1)}, u32[]{:S(2)}, u32[]{:S(2)}) collective-permute-start(bf16[4,4,16,128]{3,2,1,0:T(8,128)(2,1)S(1)} %pad_maximum_fusion.3), channel_id=1, source_target_pairs={{0,8},{4,12},{8,0},{12,4},{1,9},{5,13},{9,1},{13,5},{2,10},{6,14},... | collective-permute-start | bytes 196616 | tf_op jit(solution)/shard_map/ppermute | solution.py:80
  143.1 0.6 gather_fusion
  143.8 0.3 concatenate.56
  144.1 1.6 slice.58
  145.7 0.6 fusion.24
  146.4 0.2 collective-permute-done.2
  146.6 1.4 fusion.14
  148.0 0.2 constant_dynamic-slice_fusion
  148.3 0.1 pad_maximum_fusion.2
  148.4 0.9 fusion.29
  149.3 0.5 collective-permute-done.9
  149.8 0.3 add_convert_fusion
  150.1 0.7 copy.73
  150.8 15.8 %all-gather.5.cloned.1.call-done = bf16[3,3,3,256,128]{4,3,2,1,0:T(8,128)(2,1)} async-done(((bf16[3,3,3,32,128]{4,3,2,1,0:T(8,128)(2,1)}), bf16[3,3,3,256,128]{4,3,2,1,0:T(8,128)(2,1)}) %all-gather.5.cloned.1.call-update) | async-done | bytes 1769488 | tf_op jit(solution)/shard_map/all_gather | solution.py:69
  166.7 2.9 %copy.102 = bf16[27,256,128]{2,1,0:T(8,128)(2,1)} copy(bf16[27,256,128]{2,1,0:T(8,128)(2,1)} %bitcast.89) | data formatting | bytes 3538944
  (33 shorter events, 0.5 us)
Async XLA Ops:
  7.2 19.5 %copy-start = (bf16[27,256,128]{2,1,0:T(8,128)(2,1)S(1)}, bf16[27,256,128]{2,1,0:T(8,128)(2,1)}, u32[]{:S(2)}) copy-start(bf16[27,256,128]{2,1,0:T(8,128)(2,1)} %param.10) | copy-start | bytes 5308420
  7.2 94.3 %all-gather.3.cloned.1.call-start = ((), (), s32[]{:S(2)}) async-start(), calls=%async_computation.1 | async-start | bytes 2359296 | tf_op jit(solution)/shard_map/all_gather | solution.py:63
  11.1 15.6 %collective-permute-start = (bf16[2,2,16,8,256]{4,0,3,2,1:T(2,128)(2,1)S(1)}, bf16[2,2,16,8,256]{4,0,3,2,1:T(2,128)(2,1)S(1)}, u32[]{:S(2)}, u32[]{:S(2)}) collective-permute-start(bf16[2,2,16,8,256]{4,0,3,2,1:T(2,128)(2,1)S(1)} %slice.56), channel_id=1, source_target_pairs={{0,2},{1,3},{4,6},{5,7},{8,10},{9,11},{12,14},{13,15},{16,18},{17,... | collective-permute-start | bytes 786440 | tf_op jit(solution)/shard_map/ppermute | solution.py:13
  15.8 4.0 %collective-permute-start.3 = (bf16[1,4,16,128]{3,2,1,0:T(8,128)(2,1)}, bf16[1,4,16,128]{3,2,1,0:T(8,128)(2,1)S(1)}, u32[]{:S(2)}, u32[]{:S(2)}) collective-permute-start(bf16[1,4,16,128]{3,2,1,0:T(8,128)(2,1)} %param.15), channel_id=1, source_target_pairs={{0,4},{4,0},{8,12},{12,8},{1,5},{5,1},{9,13},{13,9},{2,6},{6,2},{1... | collective-permute-start | bytes 49160 | tf_op jit(solution)/shard_map/ppermute | solution.py:80
  20.6 4.8 %collective-permute-start.4 = (bf16[2,4,16,128]{3,2,1,0:T(8,128)(2,1)S(1)}, bf16[2,4,16,128]{3,2,1,0:T(8,128)(2,1)S(1)}, u32[]{:S(2)}, u32[]{:S(2)}) collective-permute-start(bf16[2,4,16,128]{3,2,1,0:T(8,128)(2,1)S(1)} %pad_maximum_fusion.5), channel_id=1, source_target_pairs={{0,8},{4,12},{8,0},{12,4},{1,9},{5,13},{9,1},{13,5},{2,10},{6,14},... | collective-permute-start | bytes 98312 | tf_op jit(solution)/shard_map/ppermute | solution.py:80
  26.7 7.0 %copy-start.3 = (bf16[128,16]{0,1:T(8,128)(2,1)S(1)}, bf16[128,16]{0,1:T(8,128)(2,1)}, u32[]{:S(2)}) copy-start(bf16[128,16]{0,1:T(8,128)(2,1)} %param.11) | copy-start | bytes 12292
  47.7 20.2 %all-to-all-start = ((bf16[8,2,16384]{2,1,0:T(2,128)(2,1)}), bf16[8,2,16384]{2,1,0:T(2,128)(2,1)S(1)}, u32[]{:S(2)}, u32[]{:S(2)}) async-start(bf16[8,2,16384]{2,1,0:T(2,128)(2,1)} %reshape.215), calls=%async_computation | async-start | bytes 1048576 | tf_op jit(solution)/shard_map/all_to_all | solution.py:56
  52.8 113.8 %all-gather.5.cloned.1.call-start = ((), (), s32[]{:S(2)}) async-start(), calls=%async_computation.2 | async-start | bytes 1990656 | tf_op jit(solution)/shard_map/all_gather | solution.py:69
  101.5 19.6 %copy-start.2 = (bf16[1024,128]{1,0:T(8,128)(2,1)S(1)}, bf16[1024,128]{1,0:T(8,128)(2,1)}, u32[]{:S(2)}) copy-start(bf16[1024,128]{1,0:T(8,128)(2,1)} %fusion.12) | copy-start | bytes 786436
  119.9 12.3 %collective-permute-start.5 = (f32[1,128,16]{1,2,0:T(8,128)S(1)}, f32[1,128,16]{1,2,0:T(8,128)S(1)}, u32[]{:S(2)}, u32[]{:S(2)}) collective-permute-start(f32[1,128,16]{1,2,0:T(8,128)S(1)} %convolution_bitcast_fusion), channel_id=1, source_target_pairs={{0,2},{2,0},{1,3},{3,1},{4,6},{6,4},{5,7},{7,5},{8,10},{10,8},{9,1... | collective-permute-start | bytes 24584 | tf_op jit(solution)/shard_map/ppermute | solution.py:25
  128.6 1.1 copy-start.1
  130.7 15.9 %collective-permute-start.8 = (f32[2,2,16,8,256]{4,0,3,2,1:T(2,128)}, f32[2,2,16,8,256]{4,0,3,2,1:T(2,128)S(1)}, u32[]{:S(2)}, u32[]{:S(2)}) collective-permute-start(f32[2,2,16,8,256]{4,0,3,2,1:T(2,128)} %slice.60), channel_id=1, source_target_pairs={{2,0},{3,1},{6,4},{7,5},{10,8},{11,9},{14,12},{15,13},{18,16},{19,... | collective-permute-start | bytes 1572872 | tf_op jit(solution)/shard_map/ppermute | solution.py:13
  132.2 6.1 %collective-permute-start.6 = (f32[2,128,16]{1,2,0:T(8,128)S(1)}, f32[2,128,16]{1,2,0:T(8,128)S(1)}, u32[]{:S(2)}, u32[]{:S(2)}) collective-permute-start(f32[2,128,16]{1,2,0:T(8,128)S(1)} %maximum_select_fusion.2), channel_id=1, source_target_pairs={{0,4},{4,0},{8,12},{12,8},{1,5},{5,1},{9,13},{13,9},{2,6},{6,2},{1... | collective-permute-start | bytes 49160 | tf_op jit(solution)/shard_map/ppermute | solution.py:25
  136.3 4.9 %collective-permute-start.1 = (bf16[2,4,16,128]{3,2,1,0:T(8,128)(2,1)S(1)}, bf16[2,4,16,128]{3,2,1,0:T(8,128)(2,1)S(1)}, u32[]{:S(2)}, u32[]{:S(2)}) collective-permute-start(bf16[2,4,16,128]{3,2,1,0:T(8,128)(2,1)S(1)} %reshape.186), channel_id=1, source_target_pairs={{0,4},{4,0},{8,12},{12,8},{1,5},{5,1},{9,13},{13,9},{2,6},{6,2},{1... | collective-permute-start | bytes 98312 | tf_op jit(solution)/shard_map/ppermute | solution.py:80
  138.4 7.4 %collective-permute-start.7 = (f32[4,128,16]{1,2,0:T(8,128)S(1)}, f32[4,128,16]{1,2,0:T(8,128)S(1)}, u32[]{:S(2)}, u32[]{:S(2)}) collective-permute-start(f32[4,128,16]{1,2,0:T(8,128)S(1)} %maximum_select_fusion.1), channel_id=1, source_target_pairs={{0,8},{4,12},{8,0},{12,4},{1,9},{5,13},{9,1},{13,5},{2,10},{6,14},... | collective-permute-start | bytes 98312 | tf_op jit(solution)/shard_map/ppermute | solution.py:25
  141.2 5.3 %collective-permute-start.2 = (bf16[4,4,16,128]{3,2,1,0:T(8,128)(2,1)S(1)}, bf16[4,4,16,128]{3,2,1,0:T(8,128)(2,1)S(1)}, u32[]{:S(2)}, u32[]{:S(2)}) collective-permute-start(bf16[4,4,16,128]{3,2,1,0:T(8,128)(2,1)S(1)} %pad_maximum_fusion.3), channel_id=1, source_target_pairs={{0,8},{4,12},{8,0},{12,4},{1,9},{5,13},{9,1},{13,5},{2,10},{6,14},... | collective-permute-start | bytes 196616 | tf_op jit(solution)/shard_map/ppermute | solution.py:80
  148.2 1.6 collective-permute-start.9
Sparse Core Ops, SparseCore 0:
  34.7 54.5 all-gather.2
  119.8 46.8 all-gather.4

commit v4 on v1

--- a/solution.py
+++ b/solution.py
@@ -96,8 +96,9 @@
     pad_half = KS // 2
     lat_width = proj_weight.shape[1]
     out_half = conv_weight.shape[2]
+    cache_half = shifted(video[:, frames - (KT - 1) :], "tm", 1)
     whole_now = lax.all_gather(video, "chan", axis=4, tiled=True)
-    whole_cache = shifted(whole_now[:, frames - (KT - 1) :], "tm", 1)
+    whole_cache = lax.all_gather(cache_half, "chan", axis=4, tiled=True)
     timed = jnp.concatenate([whole_cache, whole_now], axis=1)
     kernel = conv_weight.reshape(KT, KS, KS, conv_weight.shape[1], out_half)
     space_pad = [(0, 0), (pad_half, pad_half), (pad_half, pad_half)]

time: 163 us -> 162 us (level)
  blocking collectives: 5.92 us -> 7.77 us
    all_gather x0 -> x1, blocking collectives: none -> 1.99 us  [body(): whole_cache = lax.all_gather(cache_half, 'chan', axis=4, tiled=True)]
    all_gather x1, waiting for transfers between devices: 9.97 us -> 8.05 us  [weight_grad_sliced(): dpre_all = lax.all_gather(dpre5, axes, axis=0, tiled=True)]
where the time goes in v4:
time: 162 us
  waiting for transfers between devices  43.9 us (27%)
  local copies, waits for them, and re-layouts  36.2 us (22%)
  matrix products  33.5 us (21%)
  starting transfers between devices  19.3 us (12%)
  between operations  14.4 us (9%)
  blocking collectives  7.77 us (5%)
  other arithmetic  6.66 us (4%)
    conv_general_dilated x3, matrix products, conv3d(): lax.conv_general_dilated(lhs, rhs, window_strides=(1, 1, 1), padding=padd...  31 us
    all_to_all x1, waiting for transfers between devices, weight_grad_sliced(): mine = lax.all_to_all(chunks, axes, 0, 0, tiled=True)  15.2 us
    unnamed x16, local copies, waits for them, and re-layouts  15 us
    all_gather x1, waiting for transfers between devices, weight_grad_sliced(): return lax.all_gather(part, axes, axis=3, tiled=True)  13.8 us
    all_gather x1, waiting for transfers between devices, weight_grad_sliced(): dpre_all = lax.all_gather(dpre5, axes, axis=0, tiled=True)  8.05 us
    reshape x2, local copies, waits for them, and re-layouts, weight_grad_sliced(): chunks = whole_now.reshape(cam_dev, frames, height, width, count, piece)  7.18 us
    ppermute x4, waiting for transfers between devices, xor_gathered(): lax.ppermute(blocks, axis, pairs)  6.31 us
    ppermute x2, starting transfers between devices, shifted(): return lax.ppermute(shard, axis, pairs)  6.13 us
  transfers between devices with their start and end apart: 13, of which 7 were waited for; matrix products, arithmetic and copies ran while one was open for 28% of the time, Pallas kernels for 0%

profile of v4, /device:TPU:0, one launch (start us, length us, event | category | flops | bytes accessed | tf_op | source)
XLA Modules:
  0.0 161.7 jit_solution(14373492545268128435)
XLA Ops:
  7.2 1.3 copy.53
  8.6 0.1 slice.56
  8.7 4.8 %collective-permute-start = (bf16[2,2,16,8,128]{4,0,3,2,1:T(2,128)(2,1)S(1)}, bf16[2,2,16,8,128]{4,0,3,2,1:T(2,128)(2,1)S(1)}, u32[]{:S(2)}, u32[]{:S(2)}) collective-permute-start(bf16[2,2,16,8,128]{4,0,3,2,1:T(2,128)(2,1)S(1)} %slice.56), channel_id=1, source_target_pairs={{0,2},{1,3},{4,6},{5,7},{8,10},{9,11},{12,14},{13,15},{16,18},{17,... | collective-permute-start | bytes 393224 | tf_op jit(solution)/shard_map/ppermute | solution.py:13
  13.5 1.6 %collective-permute-start.3 = (bf16[1,4,16,128]{3,2,1,0:T(8,128)(2,1)}, bf16[1,4,16,128]{3,2,1,0:T(8,128)(2,1)S(1)}, u32[]{:S(2)}, u32[]{:S(2)}) collective-permute-start(bf16[1,4,16,128]{3,2,1,0:T(8,128)(2,1)} %param.15), channel_id=1, source_target_pairs={{0,4},{4,0},{8,12},{12,8},{1,5},{5,1},{9,13},{13,9},{2,6},{6,2},{1... | collective-permute-start | bytes 49160 | tf_op jit(solution)/shard_map/ppermute | solution.py:77
  15.2 2.2 %all_gather.13 = bf16[2,4,16,8,256]{4,0,3,2,1:T(2,128)(2,1)S(1)} all-gather(bf16[2,4,16,8,128]{4,0,3,2,1:T(2,128)(2,1)S(1)} %copy.53), channel_id=1, replica_groups=mesh['groups'=2,'cam'=4,'tm'=2,'chan'=2] {'chan'}, dimensions={4}, use_global_device_ids=true | all-gather | bytes 786432 | tf_op jit(solution)/shard_map/all_gather | solution.py:100
  17.3 0.8 reduce-window.8
  18.2 0.7 convert_reduce_fusion
  18.9 0.8 select_reduce_fusion.1
  19.7 0.7 pad_maximum_fusion.5
  20.4 2.6 %collective-permute-start.4 = (bf16[2,4,16,128]{3,2,1,0:T(8,128)(2,1)S(1)}, bf16[2,4,16,128]{3,2,1,0:T(8,128)(2,1)S(1)}, u32[]{:S(2)}, u32[]{:S(2)}) collective-permute-start(bf16[2,4,16,128]{3,2,1,0:T(8,128)(2,1)S(1)} %pad_maximum_fusion.5), channel_id=1, source_target_pairs={{0,8},{4,12},{8,0},{12,4},{1,9},{5,13},{9,1},{13,5},{2,10},{6,14},... | collective-permute-start | bytes 98312 | tf_op jit(solution)/shard_map/ppermute | solution.py:77
  23.0 0.1 constant_dynamic-slice_fusion.1
  23.1 0.6 gather_fusion.1
  23.7 1.8 %collective-permute-done.4 = bf16[2,4,16,128]{3,2,1,0:T(8,128)(2,1)S(1)} collective-permute-done((bf16[2,4,16,128]{3,2,1,0:T(8,128)(2,1)S(1)}, bf16[2,4,16,128]{3,2,1,0:T(8,128)(2,1)S(1)}, u32[]{:S(2)}, u32[]{:S(2)}) %collective-permute-start.4) | collective-permute-done | bytes 32800 | tf_op jit(solution)/shard_map/ppermute | solution.py:77
  25.5 0.7 pad_maximum_fusion.4
  26.2 0.3 convolution_convert_fusion
  26.5 0.2 reshape.191
  26.8 2.0 %all_gather.12 = bf16[2,2,16,8,256]{4,0,3,2,1:T(2,128)(2,1)S(1)} all-gather(bf16[2,2,16,8,128]{4,0,3,2,1:T(2,128)(2,1)S(1)} %collective-permute-done), channel_id=1, replica_groups=mesh['groups'=2,'cam'=4,'tm'=2,'chan'=2] {'chan'}, dimensions={4}, use_global_device_ids=true | all-gather | bytes 393216 | tf_op jit(solution)/shard_map/all_gather | solution.py:101
  28.8 6.6 %fusion.12 = f32[2,4,16,8,128]{4,0,3,2,1:T(2,128)S(1)} fusion(bf16[3,3,3,256,128]{4,3,2,1,0:T(8,128)(2,1)S(1)} %bitcast.82, bf16[2,4,16,8,256]{4,0,3,2,1:T(2,128)(2,1)S(1)} %all_gather.13, bf16[2,2,16,8,256]{4,0,3,2,1:T(2,128)(2,1)S(1)} %all_gather.12), kind=kOutput, calls=%fused_computation.15 | convolution fusion | flops 1593311232 | bytes 3080192 | tf_op jit(solution)/shard_map/conv_general_dilated | solution.py:37
  35.4 0.2 multiply_convert_fusion
  35.5 0.2 fusion.16
  35.8 0.3 copy-done.3
  36.1 0.9 fusion.6
  37.0 2.0 %reshape.188 = bf16[2,4,16,8,8,32]{5,4,0,3,2,1:T(8,128)(2,1)} reshape(bf16[2,4,16,8,256]{4,0,3,2,1:T(2,128)(2,1)S(1)} %all_gather.13) | data formatting | bytes 1048576 | tf_op jit(solution)/shard_map/reshape | solution.py:54
  39.0 5.1 %copy.91 = bf16[2,4,16,8,8,32]{5,0,3,2,1,4:T(2,128)(2,1)} copy(bf16[2,4,16,8,8,32]{5,4,0,3,2,1:T(8,128)(2,1)} %reshape.188) | data formatting | bytes 1048576 | tf_op jit(solution)/shard_map/reshape | solution.py:54
  44.2 5.9 %reshape.215 = bf16[8,2,16384]{2,1,0:T(2,128)(2,1)} reshape(bf16[8,4,16,8,2,32]{5,4,3,2,1,0:T(2,128)(2,1)} %bitcast.86) | data formatting | bytes 1048576
  50.1 3.9 %all-to-all-start = ((bf16[8,2,16384]{2,1,0:T(2,128)(2,1)}), bf16[8,2,16384]{2,1,0:T(2,128)(2,1)S(1)}, u32[]{:S(2)}, u32[]{:S(2)}) async-start(bf16[8,2,16384]{2,1,0:T(2,128)(2,1)} %reshape.215), calls=%async_computation | async-start | bytes 1048576 | tf_op jit(solution)/shard_map/all_to_all | solution.py:56
  54.0 0.2 all-gather.5.cloned.1.call-start
  54.3 0.1 add.90
  54.4 15.2 %all-to-all-done = bf16[8,2,16384]{2,1,0:T(2,128)(2,1)S(1)} async-done(((bf16[8,2,16384]{2,1,0:T(2,128)(2,1)}), bf16[8,2,16384]{2,1,0:T(2,128)(2,1)S(1)}, u32[]{:S(2)}, u32[]{:S(2)}) %all-to-all-start) | async-done | bytes 524320 | tf_op jit(solution)/shard_map/all_to_all | solution.py:56
  69.6 2.0 %reshape.216 = bf16[8,4,16,8,2,32]{5,4,3,2,1,0:T(2,128)(2,1)} reshape(bf16[8,2,16384]{2,1,0:T(2,128)(2,1)S(1)} %all-to-all-done) | data formatting | bytes 1048576
  71.6 5.2 %copy.60 = bf16[8,2,4,16,8,32]{5,1,0,4,3,2:T(2,128)(2,1)} copy(bf16[8,2,4,16,8,32]{5,1,4,3,2,0:T(2,128)(2,1)} %bitcast.84) | data formatting | bytes 1048576 | tf_op jit(solution)/shard_map/all_to_all | solution.py:56
  76.8 1.4 slice.57
  78.2 0.5 copy.68
  78.8 2.3 %concatenate.61 = bf16[4,2,2,2,16,8,32]{6,2,1,0,5,4,3:T(2,128)(2,1)} pad(bf16[4,1,2,2,16,8,32]{6,2,1,0,5,4,3:T(2,128)(2,1)S(1)} %copy.68, bf16[]{:T(256)} %constant.72.clone.1), padding=0_0x1_0x0_0x0_0x0_0x0_0x0_0 | pad | bytes 393218 | tf_op jit(solution)/shard_map/concatenate | solution.py:60
  81.0 8.1 %all-gather.3.cloned.1.call-done = bf16[16,4,16,8,128]{4,3,2,1,0:T(8,128)(2,1)} async-done(((bf16[2,4,16,8,128]{4,3,2,1,0:T(8,128)(2,1)}), bf16[16,4,16,8,128]{4,3,2,1,0:T(8,128)(2,1)}) %all-gather.3.cloned.1.call-update) | async-done | bytes 2097168 | tf_op jit(solution)/shard_map/all_gather | solution.py:63
  89.1 16.9 %fusion.7 = bf16[3,3,3,32,128]{4,3,2,1,0:T(8,128)(2,1)} fusion(bf16[16,4,16,8,128]{4,3,2,1,0:T(8,128)(2,1)} %all-gather.3.cloned.1.call-done, bf16[16,4,16,8,32]{4,0,3,2,1:T(8,128)(2,1)} %bitcast.87, bf16[16,2,16,8,32]{4,0,3,2,1:T(8,128)(2,1)} %bitcast.90), kind=kOutput, calls=%fused_computation.12 | convolution fusion | flops 1593421824 | bytes 3104768 | tf_op jit(solution)/shard_map/conv_general_dilated | solution.py:37
  106.1 0.2 convolution_bitcast_fusion
  106.3 0.6 collective-permute-start.5
  106.9 7.5 %fusion.19 = f32[2,6,16,8,256]{4,0,3,2,1:T(2,128)S(1)} fusion(bf16[3,3,3,256,128]{4,3,2,1,0:T(8,128)(2,1)S(1)} %bitcast.83, bf16[2,4,16,8,128]{4,3,2,1,0:T(8,128)(2,1)S(1)} %bitcast.92), kind=kOutput, calls=%fused_computation.28 | convolution fusion | flops 1591738368 | bytes 3604480 | tf_op jit(solution)/shard_map/conv_general_dilated | solution.py:37
  114.4 1.1 copy-done.1
  115.6 1.0 slice.60
  116.6 1.3 collective-permute-start.8
  117.9 0.2 fusion.33
  118.1 1.6 collective-permute-start.6
  119.6 3.6 %psum.7 = bf16[1024,16]{0,1:T(8,128)(2,1)S(1)} all-reduce(f32[1024,16]{0,1:T(8,128)S(1)} %fusion.33), channel_id=1, replica_groups=mesh['groups'=2,'cam'=4,'tm'=2,'chan'=2] {'chan'}, use_global_device_ids=true, to_apply=%region_4.5 | all-reduce | flops 16384 | bytes 98304 | tf_op jit(solution)/shard_map/psum | solution.py:110
  123.2 0.2 copy.56
  123.4 0.2 reshape.186
  123.6 0.6 collective-permute-start.1
  124.2 1.9 %collective-permute-start.7 = (f32[4,128,16]{1,2,0:T(8,128)S(1)}, f32[4,128,16]{1,2,0:T(8,128)S(1)}, u32[]{:S(2)}, u32[]{:S(2)}) collective-permute-start(f32[4,128,16]{1,2,0:T(8,128)S(1)} %maximum_select_fusion.1), channel_id=1, source_target_pairs={{0,8},{4,12},{8,0},{12,4},{1,9},{5,13},{9,1},{13,5},{2,10},{6,14},... | collective-permute-start | bytes 98312 | tf_op jit(solution)/shard_map/ppermute | solution.py:25
  126.1 2.6 %collective-permute-done.1 = bf16[2,4,16,128]{3,2,1,0:T(8,128)(2,1)S(1)} collective-permute-done((bf16[2,4,16,128]{3,2,1,0:T(8,128)(2,1)S(1)}, bf16[2,4,16,128]{3,2,1,0:T(8,128)(2,1)S(1)}, u32[]{:S(2)}, u32[]{:S(2)}) %collective-permute-start.1) | collective-permute-done | bytes 32800 | tf_op jit(solution)/shard_map/ppermute | solution.py:77
  128.8 0.6 gather_fusion
  129.4 0.3 concatenate.56
  129.7 1.6 %slice.58 = bf16[2,4,16,8,256]{4,0,3,2,1:T(2,128)(2,1)S(1)} slice(f32[2,6,16,8,256]{4,0,3,2,1:T(2,128)} %copy-done.1), slice={[0:2], [2:6], [0:16], [0:8], [0:256]} | slice | bytes 1048576 | tf_op jit(solution)/shard_map/slice | solution.py:164
  131.4 0.6 fusion.23
  132.0 1.9 %collective-permute-done.2 = bf16[4,4,16,128]{3,2,1,0:T(8,128)(2,1)S(1)} collective-permute-done((bf16[4,4,16,128]{3,2,1,0:T(8,128)(2,1)S(1)}, bf16[4,4,16,128]{3,2,1,0:T(8,128)(2,1)S(1)}, u32[]{:S(2)}, u32[]{:S(2)}) %collective-permute-start.2) | collective-permute-done | bytes 65568 | tf_op jit(solution)/shard_map/ppermute | solution.py:77
  134.0 1.4 fusion.13
  135.3 0.2 constant_dynamic-slice_fusion
  135.6 0.1 pad_maximum_fusion.2
  135.7 0.9 fusion.28
  136.6 0.5 collective-permute-done.9
  137.1 0.3 add_convert_fusion
  137.4 0.7 copy.65
  138.2 13.8 %all-gather.5.cloned.1.call-done = bf16[3,3,3,256,128]{4,3,2,1,0:T(8,128)(2,1)} async-done(((bf16[3,3,3,32,128]{4,3,2,1,0:T(8,128)(2,1)}), bf16[3,3,3,256,128]{4,3,2,1,0:T(8,128)(2,1)}) %all-gather.5.cloned.1.call-update) | async-done | bytes 1769488 | tf_op jit(solution)/shard_map/all_gather | solution.py:66
  152.0 2.9 %copy.94 = bf16[27,256,128]{2,1,0:T(8,128)(2,1)} copy(bf16[27,256,128]{2,1,0:T(8,128)(2,1)} %bitcast.88) | data formatting | bytes 3538944
  (31 shorter events, 0.5 us)
Async XLA Ops:
  7.2 21.6 %copy-start = (bf16[27,256,128]{2,1,0:T(8,128)(2,1)S(1)}, bf16[27,256,128]{2,1,0:T(8,128)(2,1)}, u32[]{:S(2)}) copy-start(bf16[27,256,128]{2,1,0:T(8,128)(2,1)} %param.10) | copy-start | bytes 5308420
  7.2 81.9 %all-gather.3.cloned.1.call-start = ((), (), s32[]{:S(2)}) async-start(), calls=%async_computation.1 | async-start | bytes 2359296 | tf_op jit(solution)/shard_map/all_gather | solution.py:63
  8.7 18.1 %collective-permute-start = (bf16[2,2,16,8,128]{4,0,3,2,1:T(2,128)(2,1)S(1)}, bf16[2,2,16,8,128]{4,0,3,2,1:T(2,128)(2,1)S(1)}, u32[]{:S(2)}, u32[]{:S(2)}) collective-permute-start(bf16[2,2,16,8,128]{4,0,3,2,1:T(2,128)(2,1)S(1)} %slice.56), channel_id=1, source_target_pairs={{0,2},{1,3},{4,6},{5,7},{8,10},{9,11},{12,14},{13,15},{16,18},{17,... | collective-permute-start | bytes 393224 | tf_op jit(solution)/shard_map/ppermute | solution.py:13
  13.5 6.2 %collective-permute-start.3 = (bf16[1,4,16,128]{3,2,1,0:T(8,128)(2,1)}, bf16[1,4,16,128]{3,2,1,0:T(8,128)(2,1)S(1)}, u32[]{:S(2)}, u32[]{:S(2)}) collective-permute-start(bf16[1,4,16,128]{3,2,1,0:T(8,128)(2,1)} %param.15), channel_id=1, source_target_pairs={{0,4},{4,0},{8,12},{12,8},{1,5},{5,1},{9,13},{13,9},{2,6},{6,2},{1... | collective-permute-start | bytes 49160 | tf_op jit(solution)/shard_map/ppermute | solution.py:77
  20.4 5.1 %collective-permute-start.4 = (bf16[2,4,16,128]{3,2,1,0:T(8,128)(2,1)S(1)}, bf16[2,4,16,128]{3,2,1,0:T(8,128)(2,1)S(1)}, u32[]{:S(2)}, u32[]{:S(2)}) collective-permute-start(bf16[2,4,16,128]{3,2,1,0:T(8,128)(2,1)S(1)} %pad_maximum_fusion.5), channel_id=1, source_target_pairs={{0,8},{4,12},{8,0},{12,4},{1,9},{5,13},{9,1},{13,5},{2,10},{6,14},... | collective-permute-start | bytes 98312 | tf_op jit(solution)/shard_map/ppermute | solution.py:77
  35.4 0.7 copy-start.3
  50.1 19.5 %all-to-all-start = ((bf16[8,2,16384]{2,1,0:T(2,128)(2,1)}), bf16[8,2,16384]{2,1,0:T(2,128)(2,1)S(1)}, u32[]{:S(2)}, u32[]{:S(2)}) async-start(bf16[8,2,16384]{2,1,0:T(2,128)(2,1)} %reshape.215), calls=%async_computation | async-start | bytes 1048576 | tf_op jit(solution)/shard_map/all_to_all | solution.py:56
  54.0 98.0 %all-gather.5.cloned.1.call-start = ((), (), s32[]{:S(2)}) async-start(), calls=%async_computation.2 | async-start | bytes 1990656 | tf_op jit(solution)/shard_map/all_gather | solution.py:66
  89.1 17.8 %copy-start.2 = (bf16[1024,128]{1,0:T(8,128)(2,1)S(1)}, bf16[1024,128]{1,0:T(8,128)(2,1)}, u32[]{:S(2)}) copy-start(bf16[1024,128]{1,0:T(8,128)(2,1)} %fusion.6) | copy-start | bytes 786436
  106.3 11.7 %collective-permute-start.5 = (f32[1,128,16]{1,2,0:T(8,128)S(1)}, f32[1,128,16]{1,2,0:T(8,128)S(1)}, u32[]{:S(2)}, u32[]{:S(2)}) collective-permute-start(f32[1,128,16]{1,2,0:T(8,128)S(1)} %convolution_bitcast_fusion), channel_id=1, source_target_pairs={{0,2},{2,0},{1,3},{3,1},{4,6},{6,4},{5,7},{7,5},{8,10},{10,8},{9,1... | collective-permute-start | bytes 24584 | tf_op jit(solution)/shard_map/ppermute | solution.py:25
  114.4 1.1 copy-start.1
  116.6 17.4 %collective-permute-start.8 = (f32[2,2,16,8,256]{4,0,3,2,1:T(2,128)}, f32[2,2,16,8,256]{4,0,3,2,1:T(2,128)S(1)}, u32[]{:S(2)}, u32[]{:S(2)}) collective-permute-start(f32[2,2,16,8,256]{4,0,3,2,1:T(2,128)} %slice.60), channel_id=1, source_target_pairs={{2,0},{3,1},{6,4},{7,5},{10,8},{11,9},{14,12},{15,13},{18,16},{19,... | collective-permute-start | bytes 1572872 | tf_op jit(solution)/shard_map/ppermute | solution.py:13
  118.1 6.1 %collective-permute-start.6 = (f32[2,128,16]{1,2,0:T(8,128)S(1)}, f32[2,128,16]{1,2,0:T(8,128)S(1)}, u32[]{:S(2)}, u32[]{:S(2)}) collective-permute-start(f32[2,128,16]{1,2,0:T(8,128)S(1)} %maximum_select_fusion.2), channel_id=1, source_target_pairs={{0,4},{4,0},{8,12},{12,8},{1,5},{5,1},{9,13},{13,9},{2,6},{6,2},{1... | collective-permute-start | bytes 49160 | tf_op jit(solution)/shard_map/ppermute | solution.py:25
  123.6 5.1 %collective-permute-start.1 = (bf16[2,4,16,128]{3,2,1,0:T(8,128)(2,1)S(1)}, bf16[2,4,16,128]{3,2,1,0:T(8,128)(2,1)S(1)}, u32[]{:S(2)}, u32[]{:S(2)}) collective-permute-start(bf16[2,4,16,128]{3,2,1,0:T(8,128)(2,1)S(1)} %reshape.186), channel_id=1, source_target_pairs={{0,4},{4,0},{8,12},{12,8},{1,5},{5,1},{9,13},{13,9},{2,6},{6,2},{1... | collective-permute-start | bytes 98312 | tf_op jit(solution)/shard_map/ppermute | solution.py:77
  124.2 7.2 %collective-permute-start.7 = (f32[4,128,16]{1,2,0:T(8,128)S(1)}, f32[4,128,16]{1,2,0:T(8,128)S(1)}, u32[]{:S(2)}, u32[]{:S(2)}) collective-permute-start(f32[4,128,16]{1,2,0:T(8,128)S(1)} %maximum_select_fusion.1), channel_id=1, source_target_pairs={{0,8},{4,12},{8,0},{12,4},{1,9},{5,13},{9,1},{13,5},{2,10},{6,14},... | collective-permute-start | bytes 98312 | tf_op jit(solution)/shard_map/ppermute | solution.py:25
  128.7 5.2 %collective-permute-start.2 = (bf16[4,4,16,128]{3,2,1,0:T(8,128)(2,1)S(1)}, bf16[4,4,16,128]{3,2,1,0:T(8,128)(2,1)S(1)}, u32[]{:S(2)}, u32[]{:S(2)}) collective-permute-start(bf16[4,4,16,128]{3,2,1,0:T(8,128)(2,1)S(1)} %pad_maximum_fusion.3), channel_id=1, source_target_pairs={{0,8},{4,12},{8,0},{12,4},{1,9},{5,13},{9,1},{13,5},{2,10},{6,14},... | collective-permute-start | bytes 196616 | tf_op jit(solution)/shard_map/ppermute | solution.py:77
  135.5 1.6 collective-permute-start.9
Sparse Core Ops, SparseCore 0:
  37.1 51.9 all-gather.2
  106.2 45.7 all-gather.4
